TPU v7x, 32 devices: a whole 2x2x4 slice. The times are simulated.
32 devices in a mesh: ens: 2 (over x), tile: 8 (over z, y), comp: 2 (over core).
Axes of the slice: x: 2, y: 2, z: 4, core: 2. Of those that a mesh axis runs over, the one named last changes fastest.
Arguments:
- increment: bfloat16 [64, 128, 256], P(('ens', 'tile'), None, 'comp'), parts along dimension 0, may hold values from -6 to 6
- land_sea: int32 [32, 128], P('tile'), may hold values 0 or 1
- kernel_x: float32 [41, 256], P(None, 'comp'), may hold values from -1 to 1
- kernel_y: float32 [41, 256], P(None, 'comp'), may hold values from -1 to 1
- balance: bfloat16 [8, 256, 256], P('tile', 'comp'), may hold values from -0.375 to 0.375
Outputs:
- filtered: bfloat16 [64, 128, 256], P('ens', 'tile', 'comp'), parts along dimension 0
There are 2 independent parts, one for each index of `ens`. A program takes and returns all parts, laid end to end along the dimension named above; an argument that names none is the same for every part. Nothing has to cross between parts.
All inputs are finite; a program needn't handle non-finite values. No bound on the sum of `land_sea` on one device may be relied on, other than what follows from the above.
Results may differ from a plain program's by a relative error of at most 0.0057.
Values may be sent and summed in bfloat16 or wider, within the bound.
No kernel may reach another device: no remote copies, remote signals or barrier semaphores. Data moves between devices by JAX's collectives and lax.ppermute only.
A program may use at most 64 MiB of HBM per device.

v0:
```python
import jax
import jax.numpy as jnp
from jax import lax
from jax.sharding import PartitionSpec as P


def zonal_filter(values, kernel):
    taps = kernel.shape[0]
    half_taps = (taps - 1) // 2
    total = jnp.zeros(values.shape, jnp.float32)
    for offset in range(taps):
        total = total + kernel[offset] * jnp.roll(values, half_taps - offset, axis=1)
    return total


def meridional_filter(values, kernel):
    taps = kernel.shape[0]
    half_taps = (taps - 1) // 2
    rows_all = values.shape[0]
    padded = jnp.pad(values, ((half_taps, half_taps), (0, 0), (0, 0)))
    total = jnp.zeros(values.shape, jnp.float32)
    for offset in range(taps):
        total = total + kernel[offset] * padded[offset : offset + rows_all]
    return total


def to_columns(row_bands):
    return lax.all_to_all(row_bands, "tile", split_axis=1, concat_axis=0, tiled=True)


def per_device(increment, land_sea, kernel_x, kernel_y, balance):
    sea = land_sea.astype(jnp.bfloat16)[:, :, None]
    masked = increment * sea
    zonal = (zonal_filter(masked, kernel_x) * sea.astype(jnp.float32)).astype(jnp.bfloat16)
    own_block = balance[0]
    mixed_rows = jnp.dot(
        lax.all_gather(zonal, "comp", axis=2, tiled=True),
        own_block.T,
        preferred_element_type=jnp.float32,
    )
    mixed = to_columns(mixed_rows.astype(jnp.bfloat16))
    return meridional_filter(mixed, kernel_y).astype(jnp.bfloat16)


def solution(mesh):
    return jax.shard_map(
        per_device,
        mesh=mesh,
        in_specs=(
            P(("ens", "tile"), None, "comp"),
            P("tile", None),
            P(None, "comp"),
            P(None, "comp"),
            P("tile", "comp", None),
        ),
        out_specs=P("ens", "tile", "comp"),
        check_vma=False,
    )
```

profile of v0, /device:TPU:0, one launch (start us, length us, event | category | flops | bytes accessed | tf_op | source)
XLA Modules:
  0.0 26.5 jit_solution(1189334224262708944)
XLA Ops:
  0.0 0.0 copy-start
  0.0 0.7 %fusion.1 = (f32[4,128]{1,0:T(4,128)S(1)}, bf16[4,128]{1,0:T(4,128)(2,1)S(1)}) fusion(s32[4,128]{1,0:T(4,128)} %param.6), kind=kLoop, calls=%fused_computation.127 | loop fusion | flops 1024 | bytes 5120 | tf_op jit(solution)/shard_map/convert_element_type | solution.py:34
  0.7 1.0 %broadcast_multiply_fusion = bf16[4,128,128]{2,1,0:T(8,128)(2,1)S(1)} fusion(bf16[4,128,128]{2,1,0:T(8,128)(2,1)} %param.5, bf16[4,128]{1,0:T(4,128)(2,1)S(1)} %get-tuple-element.6), kind=kLoop, calls=%fused_computation.44 | loop fusion | flops 65536 | bytes 263168 | tf_op jit(solution)/shard_map/mul | solution.py:33
  3.0 0.0 copy-start.2
  3.1 0.7 %copy-done.2 = f32[41,128]{1,0:T(8,128)S(1)} copy-done((f32[41,128]{1,0:T(8,128)S(1)}, f32[41,128]{1,0:T(8,128)}, u32[]{:S(2)}) %copy-start.2) | copy-done | bytes 21016
  3.8 0.0 copy-start.1
  3.8 0.9 %copy-done.1 = bf16[4,128,128]{2,1,0:T(8,128)(2,1)S(1)} copy-done((bf16[4,128,128]{2,1,0:T(8,128)(2,1)S(1)}, bf16[4,128,128]{2,1,0:T(8,128)(2,1)}, u32[]{:S(2)}) %copy-start.1) | copy-done | bytes 131096
  4.7 2.4 %multiply_convert_fusion = bf16[4,128,128]{2,1,0:T(8,128)(2,1)S(1)} fusion(bf16[4,108,128]{2,1,0:T(8,128)(2,1)S(1)} %get-tuple-element.8, bf16[4,20,128]{2,1,0:T(8,128)(2,1)S(1)} %get-tuple-element.10, bf16[4,109,128]{2,1,0:T(8,128)(2,1)S(1)} %get-tuple-element.12, bf16[4,19,128]{2,1,0:T(8,128)(2,1)S(1)} %get-tuple-element.14, ...), kind=kLoop, calls=%fused_computation.42 | loop fusion | flops 16187392 | bytes 5529088 | tf_op jit(solution)/shard_map/convert_element_type | solution.py:34
  7.1 2.1 %all_gather.3 = bf16[4,128,256]{2,1,0:T(8,128)(2,1)S(1)} all-gather(bf16[4,128,128]{2,1,0:T(8,128)(2,1)S(1)} %multiply_convert_fusion), channel_id=1, replica_groups=mesh['ens'=2,'tile'=8,'comp'=2] {'comp'}, dimensions={2}, use_global_device_ids=true | all-gather | bytes 393216 | tf_op jit(solution)/shard_map/all_gather | solution.py:37
  9.2 0.0 copy-done
  9.2 0.2 convolution_convert_fusion
  9.4 0.8 %copy.7 = bf16[4,128,128]{2,0,1:T(4,128)(2,1)} copy(bf16[4,128,128]{2,1,0:T(8,128)(2,1)S(1)} %convolution_convert_fusion) | data formatting | bytes 262144 | tf_op jit(solution)/shard_map/convert_element_type | solution.py:41
  10.2 0.0 copy-start.3
  10.2 7.3 %all-to-all-start = ((bf16[4,128,128]{2,0,1:T(4,128)(2,1)}), bf16[4,128,128]{2,0,1:T(4,128)(2,1)S(1)}, u32[]{:S(2)}, u32[]{:S(2)}) async-start(bf16[4,128,128]{2,0,1:T(4,128)(2,1)} %copy.7), calls=%async_computation | async-start | bytes 262144 | tf_op jit(solution)/shard_map/all_to_all | solution.py:28
  17.5 0.0 copy-done.3
  17.6 7.3 %all-to-all-done = bf16[4,128,128]{2,0,1:T(4,128)(2,1)S(1)} async-done(((bf16[4,128,128]{2,0,1:T(4,128)(2,1)}), bf16[4,128,128]{2,0,1:T(4,128)(2,1)S(1)}, u32[]{:S(2)}, u32[]{:S(2)}) %all-to-all-start) | async-done | bytes 131104 | tf_op jit(solution)/shard_map/all_to_all | solution.py:28
  24.9 1.6 %add_convert_fusion = bf16[32,16,128]{2,1,0:T(8,128)(2,1)} fusion(bf16[32,16,128]{2,1,0:T(8,128)(2,1)S(1)} %bitcast.174, f32[128]{0:T(128)S(1)} %get-tuple-element.126, f32[128]{0:T(128)S(1)} %get-tuple-element.127, f32[128]{0:T(128)S(1)} %get-tuple-element.88, f32[128]{0:T(128)S(1)} %get-tuple-element.89, f32[128]{0:T(128)S(1)} %get-tuple-element.90, ...), kind=kLoop, calls=%fused_computation.41 | loop fusion | flops 8060928 | bytes 283136 | tf_op jit(solution)/shard_map/convert_element_type | solution.py:42
  (47 shorter events, 1.1 us)
Async XLA Ops:
  0.0 9.2 %copy-start = (bf16[1,128,256]{2,1,0:T(8,128)(2,1)S(1)}, bf16[1,128,256]{2,1,0:T(8,128)(2,1)}, u32[]{:S(2)}) copy-start(bf16[1,128,256]{2,1,0:T(8,128)(2,1)} %param.9) | copy-start | bytes 196612
  3.0 0.7 %copy-start.2 = (f32[41,128]{1,0:T(8,128)S(1)}, f32[41,128]{1,0:T(8,128)}, u32[]{:S(2)}) copy-start(f32[41,128]{1,0:T(8,128)} %param.7) | copy-start | bytes 62980
  3.8 0.9 %copy-start.1 = (bf16[4,128,128]{2,1,0:T(8,128)(2,1)S(1)}, bf16[4,128,128]{2,1,0:T(8,128)(2,1)}, u32[]{:S(2)}) copy-start(bf16[4,128,128]{2,1,0:T(8,128)(2,1)} %param.5) | copy-start | bytes 393220
  10.2 7.3 %copy-start.3 = (f32[41,128]{1,0:T(8,128)S(1)}, f32[41,128]{1,0:T(8,128)}, u32[]{:S(2)}) copy-start(f32[41,128]{1,0:T(8,128)} %param.8) | copy-start | bytes 62980
  10.2 14.7 %all-to-all-start = ((bf16[4,128,128]{2,0,1:T(4,128)(2,1)}), bf16[4,128,128]{2,0,1:T(4,128)(2,1)S(1)}, u32[]{:S(2)}, u32[]{:S(2)}) async-start(bf16[4,128,128]{2,0,1:T(4,128)(2,1)} %copy.7), calls=%async_computation | async-start | bytes 262144 | tf_op jit(solution)/shard_map/all_to_all | solution.py:28
where the time goes:
time: 26.9 us; the launch traced here: 26.5 us
  starting transfers between devices  7.32 us (27%)
  waiting for transfers between devices  7.28 us (27%)
  other arithmetic  5.79 us (22%)
  local copies, waits for them, and re-layouts  3.41 us (13%)
  blocking collectives  2.09 us (8%)
  between operations  0.41 us (2%)
    all_to_all x1, starting transfers between devices, to_columns(): lax.all_to_all(row_bands, 'tile', split_axis=1, concat_axis=0, tiled=True)  7.32 us
    all_to_all x1, waiting for transfers between devices, to_columns(): lax.all_to_all(row_bands, 'tile', split_axis=1, concat_axis=0, tiled=True)  7.28 us
    convert_element_type x1, other arithmetic, per_device(): (zonal_filter(masked, kernel_x) * sea.astype(jnp.float32)).astype(jnp.bfl...  2.42 us
    all_gather x1, blocking collectives, per_device(): lax.all_gather(zonal, 'comp', axis=2, tiled=True)  2.09 us
    convert_element_type x1, other arithmetic, per_device(): return meridional_filter(mixed, kernel_y).astype(jnp.bfloat16)  1.63 us
    unnamed x8, local copies, waits for them, and re-layouts  1.54 us
    mul x1, other arithmetic, per_device(): masked = increment * sea  1.03 us
    slice x40, local copies, waits for them, and re-layouts, zonal_filter(): jnp.roll(values, half_taps - offset, axis=1)  1.03 us
  transfers between devices with their start and end apart: 1, of which 1 were waited for; matrix products, arithmetic and copies ran while one was open for 0% of the time, Pallas kernels for 0%

commit v1 on v0

v1 whole, which is shorter than its diff:
```python
import functools

import jax
import jax.numpy as jnp
from jax import lax
from jax.experimental import pallas as pl
from jax.experimental.pallas import tpu as pltpu
from jax.sharding import PartitionSpec as P

F32 = jnp.float32
BF16 = jnp.bfloat16


def zonal_kernel(inc_ref, sea_ref, kx_ref, out_ref, ext_ref, seat_ref):
    rows, nx, ch = inc_ref.shape
    taps = kx_ref.shape[0]
    half = (taps - 1) // 2
    pad = ((half + 7) // 8) * 8
    span = nx + 2 * pad - 8
    sea = sea_ref[...].astype(F32)
    sea_pad = jnp.concatenate([sea, jnp.zeros((128 - rows, nx), F32)], axis=0)
    seat_ref[...] = jnp.transpose(sea_pad)
    chunk = min(nx, 64)
    for r in range(rows):
        col = seat_ref[:, r : r + 1]
        m = inc_ref[r].astype(F32) * col
        ext = jnp.concatenate([m[nx - pad :], m, m[:pad]], axis=0)
        for s in range(8):
            ext_ref[s] = ext[s : s + span]

        def body(i, carry, r=r):
            x0 = pl.multiple_of(i * chunk, chunk)
            acc = jnp.zeros((chunk, ch), F32)
            for k in range(taps):
                e = k - half + pad
                q, s = divmod(e, 8)
                acc = acc + kx_ref[k : k + 1, :] * ext_ref[s, pl.ds(x0 + 8 * q, chunk), :]
            mask = seat_ref[pl.ds(x0, chunk), r : r + 1]
            out_ref[r, pl.ds(x0, chunk), :] = (acc * mask).astype(out_ref.dtype)
            return carry

        n_chunks = nx // chunk
        lax.fori_loop(0, n_chunks, body, 0, unroll=n_chunks <= 4)


def zonal(inc, sea, kx):
    rows, nx, ch = inc.shape
    taps = kx.shape[0]
    pad = (((taps - 1) // 2 + 7) // 8) * 8
    return pl.pallas_call(
        zonal_kernel,
        out_shape=jax.ShapeDtypeStruct(inc.shape, BF16),
        scratch_shapes=[
            pltpu.VMEM((8, nx + 2 * pad - 8, ch), F32),
            pltpu.VMEM((nx, 128), F32),
        ],
        cost_estimate=pl.CostEstimate(
            flops=2 * taps * inc.size, transcendentals=0, bytes_accessed=4 * inc.size
        ),
    )(inc, sea, kx)


def balance_kernel(z_ref, b_ref, out_ref):
    nt, rows, width, _ = out_ref.shape
    b = b_ref[0]
    for r in range(rows):
        res = lax.dot_general(
            z_ref[r], b, (((1,), (1,)), ((), ())), preferred_element_type=F32
        ).astype(out_ref.dtype)
        for t in range(nt):
            out_ref[t, r] = res[t * width : (t + 1) * width]


def balance_mix(z, b, nt):
    rows, nx, cj = z.shape
    ci = b.shape[1]
    return pl.pallas_call(
        balance_kernel,
        out_shape=jax.ShapeDtypeStruct((nt, rows, nx // nt, ci), BF16),
        cost_estimate=pl.CostEstimate(
            flops=2 * rows * nx * cj * ci,
            transcendentals=0,
            bytes_accessed=2 * (z.size + b.size + rows * nx * ci),
        ),
    )(z, b)


def meridional_kernel(m_ref, ky_ref, out_ref, pad_ref):
    ny, w, ch = m_ref.shape
    taps = ky_ref.shape[0]
    half = (taps - 1) // 2
    pad_ref[0:half] = jnp.zeros((half, w, ch), F32)
    pad_ref[half + ny :] = jnp.zeros((half, w, ch), F32)
    pad_ref[half : half + ny] = m_ref[...].astype(F32)
    chunk = min(ny, 8)
    n_chunks = ny // chunk

    def rows_at(y0, lo, hi):
        acc = jnp.zeros((chunk, w, ch), F32)
        for k in range(lo, hi):
            acc = acc + ky_ref[k : k + 1, :][None] * pad_ref[pl.ds(y0 + k, chunk)]
        out_ref[pl.ds(y0, chunk)] = acc.astype(out_ref.dtype)

    if n_chunks <= 8:
        for c in range(n_chunks):
            y0 = c * chunk
            lo = max(0, half - y0 - chunk + 1)
            hi = min(taps, half + ny - y0)
            rows_at(y0, lo, hi)
    else:

        def body(i, carry):
            rows_at(pl.multiple_of(i * chunk, chunk), 0, taps)
            return carry

        lax.fori_loop(0, n_chunks, body, 0)


def meridional(m, ky):
    ny, w, ch = m.shape
    taps = ky.shape[0]
    half = (taps - 1) // 2
    return pl.pallas_call(
        meridional_kernel,
        out_shape=jax.ShapeDtypeStruct(m.shape, BF16),
        scratch_shapes=[pltpu.VMEM((ny + 2 * half, w, ch), F32)],
        cost_estimate=pl.CostEstimate(
            flops=2 * taps * m.size, transcendentals=0, bytes_accessed=4 * m.size
        ),
    )(m, ky)


def per_device(nt, increment, land_sea, kernel_x, kernel_y, balance):
    z = zonal(increment, land_sea, kernel_x)
    z_all = lax.all_gather(z, "comp", axis=2, tiled=True)
    mixed = balance_mix(z_all, balance, nt)
    moved = lax.all_to_all(mixed, "tile", split_axis=0, concat_axis=0, tiled=True)
    nt_, rows, width, ch = moved.shape
    return meridional(moved.reshape(nt_ * rows, width, ch), kernel_y)


def solution(mesh):
    nt = mesh.shape["tile"]
    return jax.shard_map(
        functools.partial(per_device, nt),
        mesh=mesh,
        in_specs=(
            P(("ens", "tile"), None, "comp"),
            P("tile", None),
            P(None, "comp"),
            P(None, "comp"),
            P("tile", "comp", None),
        ),
        out_specs=P("ens", "tile", "comp"),
        check_vma=False,
    )
```

time: 26.9 us -> 25.3 us (0.941)
  blocking collectives: 2.09 us -> 18.4 us
  starting transfers between devices: 7.32 us -> 0 us
  waiting for transfers between devices: 7.28 us -> 0 us
  Pallas kernels: 0 us -> 6.6 us
  other arithmetic: 5.79 us -> 0 us
  local copies, waits for them, and re-layouts: 3.41 us -> 0 us
  between operations: 0.41 us -> 0.01 us
    all_to_all x0 -> x1, blocking collectives: none -> 14.6 us  [per_device(): lax.all_to_all(mixed, 'tile', split_axis=0, concat_axis=0, tiled=True)]
    all_to_all x1 -> x0, starting transfers between devices: 7.32 us -> none  [to_columns(): lax.all_to_all(row_bands, 'tile', split_axis=1, concat_axis=0, tiled=True)]
    all_to_all x1 -> x0, waiting for transfers between devices: 7.28 us -> none  [to_columns(): lax.all_to_all(row_bands, 'tile', split_axis=1, concat_axis=0, tiled=True)]
    pallas_call x0 -> x3, Pallas kernels: none -> 6.6 us  [the longest x1 2.65 us: zonal(): pl.pallas_call(zonal_kernel, out_shape=jax.ShapeDtypeStruct(inc.shape, BF...]
    convert_element_type x3 -> x0, other arithmetic: 4.76 us -> none  [the longest x1 2.42 us: per_device(): (zonal_filter(masked, kernel_x) * sea.astype(jnp.float32)).astype(jnp.bfl...]
    all_gather x1, blocking collectives: 2.09 us -> 3.87 us  [per_device(): z_all = lax.all_gather(z, 'comp', axis=2, tiled=True)]
    unnamed x8 -> x0, local copies, waits for them, and re-layouts: 1.54 us -> none
    mul x1 -> x0, other arithmetic: 1.03 us -> none  [per_device(): masked = increment * sea]
  transfers between devices with their start and end apart: 1 -> 0, of which waited for: 1 -> 0; matrix products, arithmetic and copies ran while one was open for 0% -> 0% of each run, Pallas kernels for 0% -> 0%
where the time goes in v1:
time: 25.3 us; the launch traced here: 25 us
  blocking collectives  18.4 us (73%)
  Pallas kernels  6.6 us (26%)
    all_to_all x1, blocking collectives, per_device(): lax.all_to_all(mixed, 'tile', split_axis=0, concat_axis=0, tiled=True)  14.6 us
    all_gather x1, blocking collectives, per_device(): z_all = lax.all_gather(z, 'comp', axis=2, tiled=True)  3.87 us
    pallas_call x1, Pallas kernels, zonal(): pl.pallas_call(zonal_kernel, out_shape=jax.ShapeDtypeStruct(inc.shape, BF...  2.65 us
    pallas_call x1, Pallas kernels, meridional(): pl.pallas_call(meridional_kernel, out_shape=jax.ShapeDtypeStruct(m.shape,...  2.12 us
    pallas_call x1, Pallas kernels, balance_mix(): pl.pallas_call(balance_kernel, out_shape=jax.ShapeDtypeStruct((nt, rows,...  1.83 us

profile of v1, /device:TPU:0, one launch (start us, length us, event | category | flops | bytes accessed | tf_op | source)
XLA Modules:
  0.0 25.0 jit_solution(8278849495395391126)
XLA Ops:
  0.0 2.6 %shard_map.55 = bf16[4,128,128]{2,1,0:T(8,128)(2,1)} custom-call(bf16[4,128,128]{2,1,0:T(8,128)(2,1)} %inc_ref.1, s32[4,128]{1,0:T(4,128)} %sea_ref.1, f32[41,128]{1,0:T(8,128)} %kx_ref.1), custom_call_target="tpu_custom_call" | custom-call | flops 5373952 | bytes 262144 | tf_op jit(solution)/shard_map/pallas_call | solution.py:50
  2.6 3.9 %all_gather.3.z_ref = bf16[4,128,256]{2,1,0:T(8,128)(2,1)} all-gather(bf16[4,128,128]{2,1,0:T(8,128)(2,1)} %shard_map.55), channel_id=1, replica_groups=mesh['ens'=2,'tile'=8,'comp'=2] {'comp'}, dimensions={2}, use_global_device_ids=true | all-gather | bytes 393216 | tf_op jit(solution)/shard_map/all_gather | solution.py:135
  6.5 1.8 %shard_map.56 = bf16[8,4,16,128]{3,2,1,0:T(8,128)(2,1)} custom-call(bf16[4,128,256]{2,1,0:T(8,128)(2,1)} %all_gather.3.z_ref, bf16[1,128,256]{2,1,0:T(8,128)(2,1)} %b_ref.1), custom_call_target="tpu_custom_call" | custom-call | flops 33554432 | bytes 458752 | tf_op jit(solution)/shard_map/pallas_call | solution.py:77
  8.4 14.6 %all_to_all.5 = bf16[8,4,16,128]{3,2,1,0:T(8,128)(2,1)} all-to-all(bf16[8,4,16,128]{3,2,1,0:T(8,128)(2,1)} %shard_map.56), channel_id=1, replica_groups=mesh['ens'=2,'tile'=8,'comp'=2] {'tile'}, dimensions={0} | all-to-all | bytes 262144 | tf_op jit(solution)/shard_map/all_to_all | solution.py:137
  22.9 2.1 %shard_map.57 = bf16[32,16,128]{2,1,0:T(8,128)(2,1)} custom-call(bf16[32,16,128]{2,1,0:T(8,128)(2,1)} %bitcast.1, f32[41,128]{1,0:T(8,128)} %ky_ref.1), custom_call_target="tpu_custom_call" | custom-call | flops 5373952 | bytes 262144 | tf_op jit(solution)/shard_map/pallas_call | solution.py:123

commit v2 on v1

--- a/solution.py
+++ b/solution.py
@@ -8,6 +8,8 @@
 from jax.sharding import PartitionSpec as P
 
 F32 = jnp.float32
+VMEM_SPEC = pl.BlockSpec(memory_space=pltpu.VMEM)
+SMALL_VMEM = pltpu.CompilerParams(vmem_limit_bytes=8 * 1024 * 1024)
 BF16 = jnp.bfloat16
 
 
@@ -50,10 +52,13 @@
     return pl.pallas_call(
         zonal_kernel,
         out_shape=jax.ShapeDtypeStruct(inc.shape, BF16),
+        in_specs=[VMEM_SPEC] * 3,
+        out_specs=VMEM_SPEC,
         scratch_shapes=[
             pltpu.VMEM((8, nx + 2 * pad - 8, ch), F32),
             pltpu.VMEM((nx, 128), F32),
         ],
+        compiler_params=SMALL_VMEM,
         cost_estimate=pl.CostEstimate(
             flops=2 * taps * inc.size, transcendentals=0, bytes_accessed=4 * inc.size
         ),
@@ -77,6 +82,9 @@
     return pl.pallas_call(
         balance_kernel,
         out_shape=jax.ShapeDtypeStruct((nt, rows, nx // nt, ci), BF16),
+        in_specs=[VMEM_SPEC] * 2,
+        out_specs=VMEM_SPEC,
+        compiler_params=SMALL_VMEM,
         cost_estimate=pl.CostEstimate(
             flops=2 * rows * nx * cj * ci,
             transcendentals=0,
@@ -123,7 +131,10 @@
     return pl.pallas_call(
         meridional_kernel,
         out_shape=jax.ShapeDtypeStruct(m.shape, BF16),
+        in_specs=[VMEM_SPEC] * 2,
+        out_specs=VMEM_SPEC,
         scratch_shapes=[pltpu.VMEM((ny + 2 * half, w, ch), F32)],
+        compiler_params=SMALL_VMEM,
         cost_estimate=pl.CostEstimate(
             flops=2 * taps * m.size, transcendentals=0, bytes_accessed=4 * m.size
         ),

time: 25.3 us -> 21.8 us (0.86)
  Pallas kernels: 6.6 us -> 2.56 us
  local copies, waits for them, and re-layouts: 0 us -> 2.33 us
  blocking collectives: 18.4 us -> 16.6 us
    unnamed x0 -> x10, local copies, waits for them, and re-layouts: none -> 2.33 us
    all_gather x1, blocking collectives: 3.87 us -> 2.22 us  [per_device(): z_all = lax.all_gather(z, 'comp', axis=2, tiled=True)]
    pallas_call x1, Pallas kernels: 1.83 us -> 0.22 us  [balance_mix(): pl.pallas_call(balance_kernel, out_shape=jax.ShapeDtypeStruct((nt, rows,...]
    pallas_call x1, Pallas kernels: 2.65 us -> 1.12 us  [zonal(): pl.pallas_call(zonal_kernel, out_shape=jax.ShapeDtypeStruct(inc.shape, BF...]
    pallas_call x1, Pallas kernels: 2.12 us -> 1.22 us  [meridional(): pl.pallas_call(meridional_kernel, out_shape=jax.ShapeDtypeStruct(m.shape,...]
where the time goes in v2:
time: 21.8 us; the launch traced here: 21.5 us
  blocking collectives  16.6 us (76%)
  Pallas kernels  2.56 us (12%)
  local copies, waits for them, and re-layouts  2.33 us (11%)
    all_to_all x1, blocking collectives, per_device(): lax.all_to_all(mixed, 'tile', split_axis=0, concat_axis=0, tiled=True)  14.3 us
    unnamed x10, local copies, waits for them, and re-layouts  2.33 us
    all_gather x1, blocking collectives, per_device(): z_all = lax.all_gather(z, 'comp', axis=2, tiled=True)  2.22 us
    pallas_call x1, Pallas kernels, meridional(): pl.pallas_call(meridional_kernel, out_shape=jax.ShapeDtypeStruct(m.shape,...  1.22 us
    pallas_call x1, Pallas kernels, zonal(): pl.pallas_call(zonal_kernel, out_shape=jax.ShapeDtypeStruct(inc.shape, BF...  1.12 us

profile of v2, /device:TPU:0, one launch (start us, length us, event | category | flops | bytes accessed | tf_op | source)
XLA Modules:
  0.0 21.5 jit_solution(10064836413315451385)
XLA Ops:
  0.0 0.0 copy-start
  0.0 0.9 %copy-done = bf16[4,128,128]{2,1,0:T(8,128)(2,1)S(1)} copy-done((bf16[4,128,128]{2,1,0:T(8,128)(2,1)S(1)}, bf16[4,128,128]{2,1,0:T(8,128)(2,1)}, u32[]{:S(2)}) %copy-start) | copy-done | bytes 131096
  0.9 0.0 copy-start.2
  0.9 0.7 %copy-done.2 = f32[41,128]{1,0:T(8,128)S(1)} copy-done((f32[41,128]{1,0:T(8,128)S(1)}, f32[41,128]{1,0:T(8,128)}, u32[]{:S(2)}) %copy-start.2) | copy-done | bytes 21016
  1.6 0.0 copy-start.4
  1.6 0.7 %copy-done.4 = s32[4,128]{1,0:T(4,128)S(1)} copy-done((s32[4,128]{1,0:T(4,128)S(1)}, s32[4,128]{1,0:T(4,128)}, u32[]{:S(2)}) %copy-start.4) | copy-done | bytes 2072
  2.3 1.1 %shard_map.55 = bf16[4,128,128]{2,1,0:T(8,128)(2,1)S(1)} custom-call(bf16[4,128,128]{2,1,0:T(8,128)(2,1)S(1)} %copy-done, s32[4,128]{1,0:T(4,128)S(1)} %copy-done.4, f32[41,128]{1,0:T(8,128)S(1)} %copy-done.2), custom_call_target="tpu_custom_call" | custom-call | flops 5373952 | bytes 262144 | tf_op jit(solution)/shard_map/pallas_call | solution.py:52
  3.4 0.0 copy-start.1
  3.5 2.2 %all_gather.3.z_ref = bf16[4,128,256]{2,1,0:T(8,128)(2,1)S(1)} all-gather(bf16[4,128,128]{2,1,0:T(8,128)(2,1)S(1)} %shard_map.55), channel_id=1, replica_groups=mesh['ens'=2,'tile'=8,'comp'=2] {'comp'}, dimensions={2}, use_global_device_ids=true | all-gather | bytes 393216 | tf_op jit(solution)/shard_map/all_gather | solution.py:146
  5.7 0.0 copy-done.1
  5.7 0.2 %shard_map.56 = bf16[8,4,16,128]{3,2,1,0:T(8,128)(2,1)S(1)} custom-call(bf16[4,128,256]{2,1,0:T(8,128)(2,1)S(1)} %all_gather.3.z_ref, bf16[1,128,256]{2,1,0:T(8,128)(2,1)S(1)} %copy-done.1), custom_call_target="tpu_custom_call" | custom-call | flops 33554432 | bytes 458752 | tf_op jit(solution)/shard_map/pallas_call | solution.py:82
  5.9 0.0 copy-start.3
  5.9 14.3 %all_to_all.5 = bf16[8,4,16,128]{3,2,1,0:T(8,128)(2,1)S(1)} all-to-all(bf16[8,4,16,128]{3,2,1,0:T(8,128)(2,1)S(1)} %shard_map.56), channel_id=1, replica_groups=mesh['ens'=2,'tile'=8,'comp'=2] {'tile'}, dimensions={0} | all-to-all | bytes 262144 | tf_op jit(solution)/shard_map/all_to_all | solution.py:148
  20.3 0.0 copy-done.3
  20.3 1.2 %shard_map.57 = bf16[32,16,128]{2,1,0:T(8,128)(2,1)} custom-call(bf16[32,16,128]{2,1,0:T(8,128)(2,1)S(1)} %bitcast.1, f32[41,128]{1,0:T(8,128)S(1)} %copy-done.3), custom_call_target="tpu_custom_call" | custom-call | flops 5373952 | bytes 262144 | tf_op jit(solution)/shard_map/pallas_call | solution.py:131
Async XLA Ops:
  0.0 0.9 %copy-start = (bf16[4,128,128]{2,1,0:T(8,128)(2,1)S(1)}, bf16[4,128,128]{2,1,0:T(8,128)(2,1)}, u32[]{:S(2)}) copy-start(bf16[4,128,128]{2,1,0:T(8,128)(2,1)} %inc_ref.1) | copy-start | bytes 393220
  0.9 0.7 %copy-start.2 = (f32[41,128]{1,0:T(8,128)S(1)}, f32[41,128]{1,0:T(8,128)}, u32[]{:S(2)}) copy-start(f32[41,128]{1,0:T(8,128)} %kx_ref.1) | copy-start | bytes 62980
  1.6 0.7 %copy-start.4 = (s32[4,128]{1,0:T(4,128)S(1)}, s32[4,128]{1,0:T(4,128)}, u32[]{:S(2)}) copy-start(s32[4,128]{1,0:T(4,128)} %sea_ref.1) | copy-start | bytes 6148
  3.4 2.2 %copy-start.1 = (bf16[1,128,256]{2,1,0:T(8,128)(2,1)S(1)}, bf16[1,128,256]{2,1,0:T(8,128)(2,1)}, u32[]{:S(2)}) copy-start(bf16[1,128,256]{2,1,0:T(8,128)(2,1)} %b_ref.1) | copy-start | bytes 196612
  5.9 14.3 %copy-start.3 = (f32[41,128]{1,0:T(8,128)S(1)}, f32[41,128]{1,0:T(8,128)}, u32[]{:S(2)}) copy-start(f32[41,128]{1,0:T(8,128)} %ky_ref.1) | copy-start | bytes 62980

commit v3 on v2

--- a/solution.py
+++ b/solution.py
@@ -13,17 +13,27 @@
 BF16 = jnp.bfloat16
 
 
-def zonal_kernel(inc_ref, sea_ref, kx_ref, out_ref, ext_ref, seat_ref):
+def zonal_kernel(inc_hbm, sea_hbm, kx_hbm, out_ref, inc_ref, sea_ref, kx_ref, ext_ref, seat_ref, sems):
     rows, nx, ch = inc_ref.shape
     taps = kx_ref.shape[0]
     half = (taps - 1) // 2
     pad = ((half + 7) // 8) * 8
     span = nx + 2 * pad - 8
+    copies = [
+        pltpu.make_async_copy(sea_hbm, sea_ref, sems.at[rows]),
+        pltpu.make_async_copy(kx_hbm, kx_ref, sems.at[rows + 1]),
+    ]
+    rows_in = [pltpu.make_async_copy(inc_hbm.at[r], inc_ref.at[r], sems.at[r]) for r in range(rows)]
+    for c in copies + rows_in:
+        c.start()
+    for c in copies:
+        c.wait()
     sea = sea_ref[...].astype(F32)
     sea_pad = jnp.concatenate([sea, jnp.zeros((128 - rows, nx), F32)], axis=0)
     seat_ref[...] = jnp.transpose(sea_pad)
     chunk = min(nx, 64)
     for r in range(rows):
+        rows_in[r].wait()
         col = seat_ref[:, r : r + 1]
         m = inc_ref[r].astype(F32) * col
         ext = jnp.concatenate([m[nx - pad :], m, m[:pad]], axis=0)
@@ -49,16 +59,20 @@
     rows, nx, ch = inc.shape
     taps = kx.shape[0]
     pad = (((taps - 1) // 2 + 7) // 8) * 8
+    any_spec = pl.BlockSpec(memory_space=pltpu.HBM)
     return pl.pallas_call(
         zonal_kernel,
         out_shape=jax.ShapeDtypeStruct(inc.shape, BF16),
-        in_specs=[VMEM_SPEC] * 3,
+        in_specs=[any_spec] * 3,
         out_specs=VMEM_SPEC,
         scratch_shapes=[
+            pltpu.VMEM(inc.shape, BF16),
+            pltpu.VMEM(sea.shape, sea.dtype),
+            pltpu.VMEM(kx.shape, F32),
             pltpu.VMEM((8, nx + 2 * pad - 8, ch), F32),
             pltpu.VMEM((nx, 128), F32),
+            pltpu.SemaphoreType.DMA((rows + 2,)),
         ],
-        compiler_params=SMALL_VMEM,
         cost_estimate=pl.CostEstimate(
             flops=2 * taps * inc.size, transcendentals=0, bytes_accessed=4 * inc.size
         ),

time: 21.8 us -> 21.4 us (0.982)
  local copies, waits for them, and re-layouts: 2.33 us -> 0.01 us
  Pallas kernels: 2.56 us -> 4.31 us
    unnamed x10 -> x4, local copies, waits for them, and re-layouts: 2.33 us -> 0.01 us
    pallas_call x1, Pallas kernels: 1.12 us -> 2.87 us  [zonal(): pl.pallas_call(zonal_kernel, out_shape=jax.ShapeDtypeStruct(inc.shape, BF...]
where the time goes in v3:
time: 21.4 us; the launch traced here: 21.1 us
  blocking collectives  16.8 us (79%)
  Pallas kernels  4.31 us (20%)
    all_to_all x1, blocking collectives, per_device(): lax.all_to_all(mixed, 'tile', split_axis=0, concat_axis=0, tiled=True)  14.3 us
    pallas_call x1, Pallas kernels, zonal(): pl.pallas_call(zonal_kernel, out_shape=jax.ShapeDtypeStruct(inc.shape, BF...  2.87 us
    all_gather x1, blocking collectives, per_device(): z_all = lax.all_gather(z, 'comp', axis=2, tiled=True)  2.43 us
    pallas_call x1, Pallas kernels, meridional(): pl.pallas_call(meridional_kernel, out_shape=jax.ShapeDtypeStruct(m.shape,...  1.22 us

profile of v3, /device:TPU:0, one launch (start us, length us, event | category | flops | bytes accessed | tf_op | source)
XLA Modules:
  0.0 21.1 jit_solution(17098188781848220882)
XLA Ops:
  0.0 2.9 %shard_map.55 = bf16[4,128,128]{2,1,0:T(8,128)(2,1)} custom-call(bf16[4,128,128]{2,1,0:T(8,128)(2,1)} %inc_hbm.1, s32[4,128]{1,0:T(4,128)} %sea_hbm.1, f32[41,128]{1,0:T(8,128)} %kx_hbm.1), custom_call_target="tpu_custom_call" | custom-call | flops 5373952 | bytes 262144 | tf_op jit(solution)/shard_map/pallas_call | solution.py:63
  2.9 0.0 copy-start
  2.9 2.4 %all_gather.3.z_ref = bf16[4,128,256]{2,1,0:T(8,128)(2,1)S(1)} all-gather(bf16[4,128,128]{2,1,0:T(8,128)(2,1)} %shard_map.55), channel_id=1, replica_groups=mesh['ens'=2,'tile'=8,'comp'=2] {'comp'}, dimensions={2}, use_global_device_ids=true | all-gather | bytes 393216 | tf_op jit(solution)/shard_map/all_gather | solution.py:160
  5.3 0.0 copy-done
  5.3 0.2 %shard_map.56 = bf16[8,4,16,128]{3,2,1,0:T(8,128)(2,1)S(1)} custom-call(bf16[4,128,256]{2,1,0:T(8,128)(2,1)S(1)} %all_gather.3.z_ref, bf16[1,128,256]{2,1,0:T(8,128)(2,1)S(1)} %copy-done), custom_call_target="tpu_custom_call" | custom-call | flops 33554432 | bytes 458752 | tf_op jit(solution)/shard_map/pallas_call | solution.py:96
  5.5 0.0 copy-start.1
  5.6 14.3 %all_to_all.5 = bf16[8,4,16,128]{3,2,1,0:T(8,128)(2,1)S(1)} all-to-all(bf16[8,4,16,128]{3,2,1,0:T(8,128)(2,1)S(1)} %shard_map.56), channel_id=1, replica_groups=mesh['ens'=2,'tile'=8,'comp'=2] {'tile'}, dimensions={0} | all-to-all | bytes 262144 | tf_op jit(solution)/shard_map/all_to_all | solution.py:162
  19.9 0.0 copy-done.1
  19.9 1.2 %shard_map.57 = bf16[32,16,128]{2,1,0:T(8,128)(2,1)} custom-call(bf16[32,16,128]{2,1,0:T(8,128)(2,1)S(1)} %bitcast.1, f32[41,128]{1,0:T(8,128)S(1)} %copy-done.1), custom_call_target="tpu_custom_call" | custom-call | flops 5373952 | bytes 262144 | tf_op jit(solution)/shard_map/pallas_call | solution.py:145
Async XLA Ops:
  2.9 2.4 %copy-start = (bf16[1,128,256]{2,1,0:T(8,128)(2,1)S(1)}, bf16[1,128,256]{2,1,0:T(8,128)(2,1)}, u32[]{:S(2)}) copy-start(bf16[1,128,256]{2,1,0:T(8,128)(2,1)} %b_ref.1) | copy-start | bytes 196612
  5.5 14.3 %copy-start.1 = (f32[41,128]{1,0:T(8,128)S(1)}, f32[41,128]{1,0:T(8,128)}, u32[]{:S(2)}) copy-start(f32[41,128]{1,0:T(8,128)} %ky_ref.1) | copy-start | bytes 62980

commit v4 on v3

--- a/solution.py
+++ b/solution.py
@@ -79,32 +79,36 @@
     )(inc, sea, kx)
 
 
-def balance_kernel(z_ref, b_ref, out_ref):
+def balance_kernel(c_ref, z_ref, zo_ref, b_ref, out_ref):
     nt, rows, width, _ = out_ref.shape
-    b = b_ref[0]
+    ch = z_ref.shape[2]
+    c = c_ref[0]
+    own = b_ref[0, :, pl.ds(pl.multiple_of(c * ch, ch), ch)]
+    other = b_ref[0, :, pl.ds(pl.multiple_of((1 - c) * ch, ch), ch)]
+    dims = (((1,), (1,)), ((), ()))
     for r in range(rows):
-        res = lax.dot_general(
-            z_ref[r], b, (((1,), (1,)), ((), ())), preferred_element_type=F32
-        ).astype(out_ref.dtype)
+        res = lax.dot_general(z_ref[r], own, dims, preferred_element_type=F32)
+        res = res + lax.dot_general(zo_ref[r], other, dims, preferred_element_type=F32)
+        res = res.astype(out_ref.dtype)
         for t in range(nt):
             out_ref[t, r] = res[t * width : (t + 1) * width]
 
 
-def balance_mix(z, b, nt):
-    rows, nx, cj = z.shape
+def balance_mix(c, z, zo, b, nt):
+    rows, nx, ch = z.shape
     ci = b.shape[1]
     return pl.pallas_call(
         balance_kernel,
         out_shape=jax.ShapeDtypeStruct((nt, rows, nx // nt, ci), BF16),
-        in_specs=[VMEM_SPEC] * 2,
+        in_specs=[pl.BlockSpec(memory_space=pltpu.SMEM)] + [VMEM_SPEC] * 3,
         out_specs=VMEM_SPEC,
         compiler_params=SMALL_VMEM,
         cost_estimate=pl.CostEstimate(
-            flops=2 * rows * nx * cj * ci,
+            flops=4 * rows * nx * ch * ci,
             transcendentals=0,
-            bytes_accessed=2 * (z.size + b.size + rows * nx * ci),
+            bytes_accessed=2 * (2 * z.size + b.size + rows * nx * ci),
         ),
-    )(z, b)
+    )(c, z, zo, b)
 
 
 def meridional_kernel(m_ref, ky_ref, out_ref, pad_ref):
@@ -157,8 +161,9 @@
 
 def per_device(nt, increment, land_sea, kernel_x, kernel_y, balance):
     z = zonal(increment, land_sea, kernel_x)
-    z_all = lax.all_gather(z, "comp", axis=2, tiled=True)
-    mixed = balance_mix(z_all, balance, nt)
+    z_other = lax.ppermute(z, "comp", [(0, 1), (1, 0)])
+    c = lax.axis_index("comp").astype(jnp.int32).reshape(1)
+    mixed = balance_mix(c, z, z_other, balance, nt)
     moved = lax.all_to_all(mixed, "tile", split_axis=0, concat_axis=0, tiled=True)
     nt_, rows, width, ch = moved.shape
     return meridional(moved.reshape(nt_ * rows, width, ch), kernel_y)

time: 21.4 us -> 21.7 us (1.014)
  blocking collectives: 16.8 us -> 14.3 us
  waiting for transfers between devices: 0 us -> 1.2 us
  local copies, waits for them, and re-layouts: 0.01 us -> 0.91 us
  starting transfers between devices: 0 us -> 0.52 us
    all_gather x1 -> x0, blocking collectives: 2.43 us -> none  [per_device(): z_all = lax.all_gather(z, 'comp', axis=2, tiled=True)]
    ppermute x0 -> x1, waiting for transfers between devices: none -> 1.2 us  [per_device(): z_other = lax.ppermute(z, 'comp', [(0, 1), (1, 0)])]
    unnamed x4 -> x6, local copies, waits for them, and re-layouts: 0.01 us -> 0.91 us
    ppermute x0 -> x1, starting transfers between devices: none -> 0.52 us  [per_device(): z_other = lax.ppermute(z, 'comp', [(0, 1), (1, 0)])]
  transfers between devices with their start and end apart: 0 -> 1, of which waited for: 0 -> 1; matrix products, arithmetic and copies ran while one was open for 0% -> 0% of each run, Pallas kernels for 0% -> 0%
where the time goes in v4:
time: 21.7 us; the launch traced here: 21.4 us
  blocking collectives  14.3 us (66%)
  Pallas kernels  4.41 us (20%)
  waiting for transfers between devices  1.2 us (6%)
  local copies, waits for them, and re-layouts  0.91 us (4%)
  starting transfers between devices  0.52 us (2%)
    all_to_all x1, blocking collectives, per_device(): lax.all_to_all(mixed, 'tile', split_axis=0, concat_axis=0, tiled=True)  14.3 us
    pallas_call x1, Pallas kernels, zonal(): pl.pallas_call(zonal_kernel, out_shape=jax.ShapeDtypeStruct(inc.shape, BF...  2.9 us
    pallas_call x1, Pallas kernels, meridional(): pl.pallas_call(meridional_kernel, out_shape=jax.ShapeDtypeStruct(m.shape,...  1.22 us
    ppermute x1, waiting for transfers between devices, per_device(): z_other = lax.ppermute(z, 'comp', [(0, 1), (1, 0)])  1.2 us
    unnamed x6, local copies, waits for them, and re-layouts  0.91 us
    ppermute x1, starting transfers between devices, per_device(): z_other = lax.ppermute(z, 'comp', [(0, 1), (1, 0)])  0.52 us
  transfers between devices with their start and end apart: 1, of which 1 were waited for; matrix products, arithmetic and copies ran while one was open for 0% of the time, Pallas kernels for 0%

profile of v4, /device:TPU:0, one launch (start us, length us, event | category | flops | bytes accessed | tf_op | source)
XLA Modules:
  0.0 21.4 jit_solution(14154192178463230625)
XLA Ops:
  0.0 0.0 copy-start.1
  0.0 2.9 %shard_map.55.z_ref = bf16[4,128,128]{2,1,0:T(8,128)(2,1)} custom-call(bf16[4,128,128]{2,1,0:T(8,128)(2,1)} %inc_hbm.1, s32[4,128]{1,0:T(4,128)} %sea_hbm.1, f32[41,128]{1,0:T(8,128)} %kx_hbm.1), custom_call_target="tpu_custom_call" | custom-call | flops 5373952 | bytes 262144 | tf_op jit(solution)/shard_map/pallas_call | solution.py:63
  2.9 0.5 %collective-permute-start = (bf16[4,128,128]{2,1,0:T(8,128)(2,1)}, bf16[4,128,128]{2,1,0:T(8,128)(2,1)S(1)}, u32[]{:S(2)}, u32[]{:S(2)}) collective-permute-start(bf16[4,128,128]{2,1,0:T(8,128)(2,1)} %shard_map.55.z_ref), channel_id=1, source_target_pairs={{0,1},{1,0},{2,3},{3,2},{4,5},{5,4},{6,7},{7,6},{8,9},{9,8},{10,11... | collective-permute-start | bytes 393224 | tf_op jit(solution)/shard_map/ppermute | solution.py:164
  3.4 1.2 %collective-permute-done.zo_ref = bf16[4,128,128]{2,1,0:T(8,128)(2,1)S(1)} collective-permute-done((bf16[4,128,128]{2,1,0:T(8,128)(2,1)}, bf16[4,128,128]{2,1,0:T(8,128)(2,1)S(1)}, u32[]{:S(2)}, u32[]{:S(2)}) %collective-permute-start) | collective-permute-done | bytes 131104 | tf_op jit(solution)/shard_map/ppermute | solution.py:164
  4.6 0.0 copy-done.1
  4.6 0.0 copy-start
  4.6 0.9 %copy-done = bf16[4,128,128]{2,1,0:T(8,128)(2,1)S(1)} copy-done((bf16[4,128,128]{2,1,0:T(8,128)(2,1)S(1)}, bf16[4,128,128]{2,1,0:T(8,128)(2,1)}, u32[]{:S(2)}) %copy-start) | copy-done | bytes 131096
  5.5 0.3 %shard_map.56 = bf16[8,4,16,128]{3,2,1,0:T(8,128)(2,1)S(1)} custom-call(s32[1]{0:T(128)} %bitcast.c_ref, bf16[4,128,128]{2,1,0:T(8,128)(2,1)S(1)} %copy-done, bf16[4,128,128]{2,1,0:T(8,128)(2,1)S(1)} %collective-permute-done.zo_ref, bf16[1,128,256]{2,1,0:T(8,128)(2,1)S(1)} %copy-done.1), custom_call_target="tpu_custom_call" | custom-call | flops 33554432 | bytes 458752 | tf_op jit(solution)/shard_map/pallas_call | solution.py:100
  5.8 0.0 copy-start.2
  5.8 14.3 %all_to_all.5 = bf16[8,4,16,128]{3,2,1,0:T(8,128)(2,1)S(1)} all-to-all(bf16[8,4,16,128]{3,2,1,0:T(8,128)(2,1)S(1)} %shard_map.56), channel_id=1, replica_groups=mesh['ens'=2,'tile'=8,'comp'=2] {'tile'}, dimensions={0} | all-to-all | bytes 262144 | tf_op jit(solution)/shard_map/all_to_all | solution.py:167
  20.2 0.0 copy-done.2
  20.2 1.2 %shard_map.57 = bf16[32,16,128]{2,1,0:T(8,128)(2,1)} custom-call(bf16[32,16,128]{2,1,0:T(8,128)(2,1)S(1)} %bitcast.2, f32[41,128]{1,0:T(8,128)S(1)} %copy-done.2), custom_call_target="tpu_custom_call" | custom-call | flops 5373952 | bytes 262144 | tf_op jit(solution)/shard_map/pallas_call | solution.py:149
Async XLA Ops:
  0.0 4.6 %copy-start.1 = (bf16[1,128,256]{2,1,0:T(8,128)(2,1)S(1)}, bf16[1,128,256]{2,1,0:T(8,128)(2,1)}, u32[]{:S(2)}) copy-start(bf16[1,128,256]{2,1,0:T(8,128)(2,1)} %b_ref.1) | copy-start | bytes 196612
  2.9 1.7 %collective-permute-start = (bf16[4,128,128]{2,1,0:T(8,128)(2,1)}, bf16[4,128,128]{2,1,0:T(8,128)(2,1)S(1)}, u32[]{:S(2)}, u32[]{:S(2)}) collective-permute-start(bf16[4,128,128]{2,1,0:T(8,128)(2,1)} %shard_map.55.z_ref), channel_id=1, source_target_pairs={{0,1},{1,0},{2,3},{3,2},{4,5},{5,4},{6,7},{7,6},{8,9},{9,8},{10,11... | collective-permute-start | bytes 393224 | tf_op jit(solution)/shard_map/ppermute | solution.py:164
  4.6 0.9 %copy-start = (bf16[4,128,128]{2,1,0:T(8,128)(2,1)S(1)}, bf16[4,128,128]{2,1,0:T(8,128)(2,1)}, u32[]{:S(2)}) copy-start(bf16[4,128,128]{2,1,0:T(8,128)(2,1)} %shard_map.55.z_ref) | copy-start | bytes 393220
  5.8 14.3 %copy-start.2 = (f32[41,128]{1,0:T(8,128)S(1)}, f32[41,128]{1,0:T(8,128)}, u32[]{:S(2)}) copy-start(f32[41,128]{1,0:T(8,128)} %ky_ref.1) | copy-start | bytes 62980

commit v5 on v4

--- a/solution.py
+++ b/solution.py
@@ -13,27 +13,17 @@
 BF16 = jnp.bfloat16
 
 
-def zonal_kernel(inc_hbm, sea_hbm, kx_hbm, out_ref, inc_ref, sea_ref, kx_ref, ext_ref, seat_ref, sems):
+def zonal_kernel(inc_ref, sea_ref, kx_ref, out_ref, ext_ref, seat_ref):
     rows, nx, ch = inc_ref.shape
     taps = kx_ref.shape[0]
     half = (taps - 1) // 2
     pad = ((half + 7) // 8) * 8
     span = nx + 2 * pad - 8
-    copies = [
-        pltpu.make_async_copy(sea_hbm, sea_ref, sems.at[rows]),
-        pltpu.make_async_copy(kx_hbm, kx_ref, sems.at[rows + 1]),
-    ]
-    rows_in = [pltpu.make_async_copy(inc_hbm.at[r], inc_ref.at[r], sems.at[r]) for r in range(rows)]
-    for c in copies + rows_in:
-        c.start()
-    for c in copies:
-        c.wait()
     sea = sea_ref[...].astype(F32)
     sea_pad = jnp.concatenate([sea, jnp.zeros((128 - rows, nx), F32)], axis=0)
     seat_ref[...] = jnp.transpose(sea_pad)
     chunk = min(nx, 64)
     for r in range(rows):
-        rows_in[r].wait()
         col = seat_ref[:, r : r + 1]
         m = inc_ref[r].astype(F32) * col
         ext = jnp.concatenate([m[nx - pad :], m, m[:pad]], axis=0)
@@ -59,20 +49,16 @@
     rows, nx, ch = inc.shape
     taps = kx.shape[0]
     pad = (((taps - 1) // 2 + 7) // 8) * 8
-    any_spec = pl.BlockSpec(memory_space=pltpu.HBM)
     return pl.pallas_call(
         zonal_kernel,
         out_shape=jax.ShapeDtypeStruct(inc.shape, BF16),
-        in_specs=[any_spec] * 3,
+        in_specs=[VMEM_SPEC] * 3,
         out_specs=VMEM_SPEC,
         scratch_shapes=[
-            pltpu.VMEM(inc.shape, BF16),
-            pltpu.VMEM(sea.shape, sea.dtype),
-            pltpu.VMEM(kx.shape, F32),
             pltpu.VMEM((8, nx + 2 * pad - 8, ch), F32),
             pltpu.VMEM((nx, 128), F32),
-            pltpu.SemaphoreType.DMA((rows + 2,)),
         ],
+        compiler_params=SMALL_VMEM,
         cost_estimate=pl.CostEstimate(
             flops=2 * taps * inc.size, transcendentals=0, bytes_accessed=4 * inc.size
         ),

time: 21.7 us -> 21.1 us (0.972)
  Pallas kernels: 4.41 us -> 2.57 us
  local copies, waits for them, and re-layouts: 0.91 us -> 2.33 us
    pallas_call x1, Pallas kernels: 2.9 us -> 1.06 us  [zonal(): pl.pallas_call(zonal_kernel, out_shape=jax.ShapeDtypeStruct(inc.shape, BF...]
    unnamed x6 -> x10, local copies, waits for them, and re-layouts: 0.91 us -> 2.33 us
where the time goes in v5:
time: 21.1 us; the launch traced here: 20.8 us
  blocking collectives  14.3 us (68%)
  Pallas kernels  2.57 us (12%)
  local copies, waits for them, and re-layouts  2.33 us (11%)
  waiting for transfers between devices  0.99 us (5%)
  starting transfers between devices  0.52 us (2%)
    all_to_all x1, blocking collectives, per_device(): lax.all_to_all(mixed, 'tile', split_axis=0, concat_axis=0, tiled=True)  14.3 us
    unnamed x10, local copies, waits for them, and re-layouts  2.33 us
    pallas_call x1, Pallas kernels, meridional(): pl.pallas_call(meridional_kernel, out_shape=jax.ShapeDtypeStruct(m.shape,...  1.22 us
    pallas_call x1, Pallas kernels, zonal(): pl.pallas_call(zonal_kernel, out_shape=jax.ShapeDtypeStruct(inc.shape, BF...  1.06 us
    ppermute x1, waiting for transfers between devices, per_device(): z_other = lax.ppermute(z, 'comp', [(0, 1), (1, 0)])  0.99 us
    ppermute x1, starting transfers between devices, per_device(): z_other = lax.ppermute(z, 'comp', [(0, 1), (1, 0)])  0.52 us
  transfers between devices with their start and end apart: 1, of which 1 were waited for; matrix products, arithmetic and copies ran while one was open for 0% of the time, Pallas kernels for 0%

profile of v5, /device:TPU:0, one launch (start us, length us, event | category | flops | bytes accessed | tf_op | source)
XLA Modules:
  0.0 20.8 jit_solution(16430678971948297105)
XLA Ops:
  0.0 0.0 copy-start
  0.0 0.9 %copy-done = bf16[4,128,128]{2,1,0:T(8,128)(2,1)S(1)} copy-done((bf16[4,128,128]{2,1,0:T(8,128)(2,1)S(1)}, bf16[4,128,128]{2,1,0:T(8,128)(2,1)}, u32[]{:S(2)}) %copy-start) | copy-done | bytes 131096
  0.9 0.0 copy-start.2
  0.9 0.7 %copy-done.2 = f32[41,128]{1,0:T(8,128)S(1)} copy-done((f32[41,128]{1,0:T(8,128)S(1)}, f32[41,128]{1,0:T(8,128)}, u32[]{:S(2)}) %copy-start.2) | copy-done | bytes 21016
  1.6 0.0 copy-start.4
  1.6 0.7 %copy-done.4 = s32[4,128]{1,0:T(4,128)S(1)} copy-done((s32[4,128]{1,0:T(4,128)S(1)}, s32[4,128]{1,0:T(4,128)}, u32[]{:S(2)}) %copy-start.4) | copy-done | bytes 2072
  2.3 0.0 copy-start.1
  2.3 1.1 %shard_map.55.z_ref = bf16[4,128,128]{2,1,0:T(8,128)(2,1)S(1)} custom-call(bf16[4,128,128]{2,1,0:T(8,128)(2,1)S(1)} %copy-done, s32[4,128]{1,0:T(4,128)S(1)} %copy-done.4, f32[41,128]{1,0:T(8,128)S(1)} %copy-done.2), custom_call_target="tpu_custom_call" | custom-call | flops 5373952 | bytes 262144 | tf_op jit(solution)/shard_map/pallas_call | solution.py:52
  3.4 0.5 %collective-permute-start = (bf16[4,128,128]{2,1,0:T(8,128)(2,1)S(1)}, bf16[4,128,128]{2,1,0:T(8,128)(2,1)S(1)}, u32[]{:S(2)}, u32[]{:S(2)}) collective-permute-start(bf16[4,128,128]{2,1,0:T(8,128)(2,1)S(1)} %shard_map.55.z_ref), channel_id=1, source_target_pairs={{0,1},{1,0},{2,3},{3,2},{4,5},{5,4},{6,7},{7,6},{8,9},{9,8},{10,11... | collective-permute-start | bytes 393224 | tf_op jit(solution)/shard_map/ppermute | solution.py:150
  3.9 1.0 %collective-permute-done.zo_ref = bf16[4,128,128]{2,1,0:T(8,128)(2,1)S(1)} collective-permute-done((bf16[4,128,128]{2,1,0:T(8,128)(2,1)S(1)}, bf16[4,128,128]{2,1,0:T(8,128)(2,1)S(1)}, u32[]{:S(2)}, u32[]{:S(2)}) %collective-permute-start) | collective-permute-done | bytes 131104 | tf_op jit(solution)/shard_map/ppermute | solution.py:150
  4.9 0.0 copy-done.1
  4.9 0.3 %shard_map.56 = bf16[8,4,16,128]{3,2,1,0:T(8,128)(2,1)S(1)} custom-call(s32[1]{0:T(128)} %bitcast.c_ref, bf16[4,128,128]{2,1,0:T(8,128)(2,1)S(1)} %shard_map.55.z_ref, bf16[4,128,128]{2,1,0:T(8,128)(2,1)S(1)} %collective-permute-done.zo_ref, bf16[1,128,256]{2,1,0:T(8,128)(2,1)S(1)} %copy-done.1), custom_call_target="tpu_custom_call" | custom-call | flops 33554432 | bytes 458752 | tf_op jit(solution)/shard_map/pallas_call | solution.py:86
  5.2 0.0 copy-start.3
  5.2 14.3 %all_to_all.5 = bf16[8,4,16,128]{3,2,1,0:T(8,128)(2,1)S(1)} all-to-all(bf16[8,4,16,128]{3,2,1,0:T(8,128)(2,1)S(1)} %shard_map.56), channel_id=1, replica_groups=mesh['ens'=2,'tile'=8,'comp'=2] {'tile'}, dimensions={0} | all-to-all | bytes 262144 | tf_op jit(solution)/shard_map/all_to_all | solution.py:153
  19.5 0.0 copy-done.3
  19.6 1.2 %shard_map.57 = bf16[32,16,128]{2,1,0:T(8,128)(2,1)} custom-call(bf16[32,16,128]{2,1,0:T(8,128)(2,1)S(1)} %bitcast.2, f32[41,128]{1,0:T(8,128)S(1)} %copy-done.3), custom_call_target="tpu_custom_call" | custom-call | flops 5373952 | bytes 262144 | tf_op jit(solution)/shard_map/pallas_call | solution.py:135
Async XLA Ops:
  0.0 0.9 %copy-start = (bf16[4,128,128]{2,1,0:T(8,128)(2,1)S(1)}, bf16[4,128,128]{2,1,0:T(8,128)(2,1)}, u32[]{:S(2)}) copy-start(bf16[4,128,128]{2,1,0:T(8,128)(2,1)} %inc_ref.1) | copy-start | bytes 393220
  0.9 0.7 %copy-start.2 = (f32[41,128]{1,0:T(8,128)S(1)}, f32[41,128]{1,0:T(8,128)}, u32[]{:S(2)}) copy-start(f32[41,128]{1,0:T(8,128)} %kx_ref.1) | copy-start | bytes 62980
  1.6 0.7 %copy-start.4 = (s32[4,128]{1,0:T(4,128)S(1)}, s32[4,128]{1,0:T(4,128)}, u32[]{:S(2)}) copy-start(s32[4,128]{1,0:T(4,128)} %sea_ref.1) | copy-start | bytes 6148
  2.3 2.6 %copy-start.1 = (bf16[1,128,256]{2,1,0:T(8,128)(2,1)S(1)}, bf16[1,128,256]{2,1,0:T(8,128)(2,1)}, u32[]{:S(2)}) copy-start(bf16[1,128,256]{2,1,0:T(8,128)(2,1)} %b_ref.1) | copy-start | bytes 196612
  3.4 1.5 %collective-permute-start = (bf16[4,128,128]{2,1,0:T(8,128)(2,1)S(1)}, bf16[4,128,128]{2,1,0:T(8,128)(2,1)S(1)}, u32[]{:S(2)}, u32[]{:S(2)}) collective-permute-start(bf16[4,128,128]{2,1,0:T(8,128)(2,1)S(1)} %shard_map.55.z_ref), channel_id=1, source_target_pairs={{0,1},{1,0},{2,3},{3,2},{4,5},{5,4},{6,7},{7,6},{8,9},{9,8},{10,11... | collective-permute-start | bytes 393224 | tf_op jit(solution)/shard_map/ppermute | solution.py:150
  5.2 14.4 %copy-start.3 = (f32[41,128]{1,0:T(8,128)S(1)}, f32[41,128]{1,0:T(8,128)}, u32[]{:S(2)}) copy-start(f32[41,128]{1,0:T(8,128)} %ky_ref.1) | copy-start | bytes 62980

commit v6 on v5

--- a/solution.py
+++ b/solution.py
@@ -13,19 +13,15 @@
 BF16 = jnp.bfloat16
 
 
-def zonal_kernel(inc_ref, sea_ref, kx_ref, out_ref, ext_ref, seat_ref):
-    rows, nx, ch = inc_ref.shape
+def zonal_kernel(m_ref, kx_ref, out_ref, ext_ref):
+    rows, nx, ch = m_ref.shape
     taps = kx_ref.shape[0]
     half = (taps - 1) // 2
     pad = ((half + 7) // 8) * 8
     span = nx + 2 * pad - 8
-    sea = sea_ref[...].astype(F32)
-    sea_pad = jnp.concatenate([sea, jnp.zeros((128 - rows, nx), F32)], axis=0)
-    seat_ref[...] = jnp.transpose(sea_pad)
     chunk = min(nx, 64)
     for r in range(rows):
-        col = seat_ref[:, r : r + 1]
-        m = inc_ref[r].astype(F32) * col
+        m = m_ref[r].astype(F32)
         ext = jnp.concatenate([m[nx - pad :], m, m[:pad]], axis=0)
         for s in range(8):
             ext_ref[s] = ext[s : s + span]
@@ -37,37 +33,36 @@
                 e = k - half + pad
                 q, s = divmod(e, 8)
                 acc = acc + kx_ref[k : k + 1, :] * ext_ref[s, pl.ds(x0 + 8 * q, chunk), :]
-            mask = seat_ref[pl.ds(x0, chunk), r : r + 1]
-            out_ref[r, pl.ds(x0, chunk), :] = (acc * mask).astype(out_ref.dtype)
+            out_ref[r, pl.ds(x0, chunk), :] = acc.astype(out_ref.dtype)
             return carry
 
         n_chunks = nx // chunk
         lax.fori_loop(0, n_chunks, body, 0, unroll=n_chunks <= 4)
 
 
-def zonal(inc, sea, kx):
-    rows, nx, ch = inc.shape
+def zonal(m, kx):
+    rows, nx, ch = m.shape
     taps = kx.shape[0]
     pad = (((taps - 1) // 2 + 7) // 8) * 8
     return pl.pallas_call(
         zonal_kernel,
-        out_shape=jax.ShapeDtypeStruct(inc.shape, BF16),
-        in_specs=[VMEM_SPEC] * 3,
+        out_shape=jax.ShapeDtypeStruct(m.shape, BF16),
+        in_specs=[VMEM_SPEC] * 2,
         out_specs=VMEM_SPEC,
-        scratch_shapes=[
-            pltpu.VMEM((8, nx + 2 * pad - 8, ch), F32),
-            pltpu.VMEM((nx, 128), F32),
-        ],
+        scratch_shapes=[pltpu.VMEM((8, nx + 2 * pad - 8, ch), F32)],
         compiler_params=SMALL_VMEM,
         cost_estimate=pl.CostEstimate(
-            flops=2 * taps * inc.size, transcendentals=0, bytes_accessed=4 * inc.size
+            flops=2 * taps * m.size, transcendentals=0, bytes_accessed=4 * m.size
         ),
-    )(inc, sea, kx)
+    )(m, kx)
 
 
-def balance_kernel(c_ref, z_ref, zo_ref, b_ref, out_ref):
+def balance_kernel(c_ref, z_ref, zo_ref, b_ref, sea_ref, out_ref, seat_ref):
     nt, rows, width, _ = out_ref.shape
-    ch = z_ref.shape[2]
+    nx, ch = z_ref.shape[1], z_ref.shape[2]
+    sea = sea_ref[...].astype(F32)
+    sea_pad = jnp.concatenate([sea, jnp.zeros((128 - rows, nx), F32)], axis=0)
+    seat_ref[...] = jnp.transpose(sea_pad)
     c = c_ref[0]
     own = b_ref[0, :, pl.ds(pl.multiple_of(c * ch, ch), ch)]
     other = b_ref[0, :, pl.ds(pl.multiple_of((1 - c) * ch, ch), ch)]
@@ -75,26 +70,27 @@
     for r in range(rows):
         res = lax.dot_general(z_ref[r], own, dims, preferred_element_type=F32)
         res = res + lax.dot_general(zo_ref[r], other, dims, preferred_element_type=F32)
-        res = res.astype(out_ref.dtype)
+        res = (res * seat_ref[:, r : r + 1]).astype(out_ref.dtype)
         for t in range(nt):
             out_ref[t, r] = res[t * width : (t + 1) * width]
 
 
-def balance_mix(c, z, zo, b, nt):
+def balance_mix(c, z, zo, b, sea, nt):
     rows, nx, ch = z.shape
     ci = b.shape[1]
     return pl.pallas_call(
         balance_kernel,
         out_shape=jax.ShapeDtypeStruct((nt, rows, nx // nt, ci), BF16),
-        in_specs=[pl.BlockSpec(memory_space=pltpu.SMEM)] + [VMEM_SPEC] * 3,
+        in_specs=[pl.BlockSpec(memory_space=pltpu.SMEM)] + [VMEM_SPEC] * 4,
         out_specs=VMEM_SPEC,
+        scratch_shapes=[pltpu.VMEM((nx, 128), F32)],
         compiler_params=SMALL_VMEM,
         cost_estimate=pl.CostEstimate(
             flops=4 * rows * nx * ch * ci,
             transcendentals=0,
             bytes_accessed=2 * (2 * z.size + b.size + rows * nx * ci),
         ),
-    )(c, z, zo, b)
+    )(c, z, zo, b, sea)
 
 
 def meridional_kernel(m_ref, ky_ref, out_ref, pad_ref):
@@ -146,10 +142,11 @@
 
 
 def per_device(nt, increment, land_sea, kernel_x, kernel_y, balance):
-    z = zonal(increment, land_sea, kernel_x)
+    masked = increment * land_sea.astype(increment.dtype)[:, :, None]
+    z = zonal(masked, kernel_x)
     z_other = lax.ppermute(z, "comp", [(0, 1), (1, 0)])
     c = lax.axis_index("comp").astype(jnp.int32).reshape(1)
-    mixed = balance_mix(c, z, z_other, balance, nt)
+    mixed = balance_mix(c, z, z_other, balance, land_sea, nt)
     moved = lax.all_to_all(mixed, "tile", split_axis=0, concat_axis=0, tiled=True)
     nt_, rows, width, ch = moved.shape
     return meridional(moved.reshape(nt_ * rows, width, ch), kernel_y)

time: 21.1 us -> 20.3 us (0.962)
  local copies, waits for them, and re-layouts: 2.33 us -> 0.02 us
  other arithmetic: 0 us -> 1.72 us
    unnamed x10 -> x8, local copies, waits for them, and re-layouts: 2.33 us -> 0.02 us
    mul x0 -> x1, other arithmetic: none -> 1.04 us  [per_device(): masked = increment * land_sea.astype(increment.dtype)[:, :, None]]
    convert_element_type x0 -> x1, other arithmetic: none -> 0.68 us  [per_device(): masked = increment * land_sea.astype(increment.dtype)[:, :, None]]
where the time goes in v6:
time: 20.3 us; the launch traced here: 20.1 us
  blocking collectives  14.3 us (70%)
  Pallas kernels  2.43 us (12%)
  other arithmetic  1.72 us (8%)
  waiting for transfers between devices  0.98 us (5%)
  starting transfers between devices  0.52 us (3%)
    all_to_all x1, blocking collectives, per_device(): lax.all_to_all(mixed, 'tile', split_axis=0, concat_axis=0, tiled=True)  14.3 us
    pallas_call x1, Pallas kernels, meridional(): pl.pallas_call(meridional_kernel, out_shape=jax.ShapeDtypeStruct(m.shape,...  1.22 us
    mul x1, other arithmetic, per_device(): masked = increment * land_sea.astype(increment.dtype)[:, :, None]  1.04 us
    ppermute x1, waiting for transfers between devices, per_device(): z_other = lax.ppermute(z, 'comp', [(0, 1), (1, 0)])  0.98 us
    pallas_call x1, Pallas kernels, zonal(): pl.pallas_call(zonal_kernel, out_shape=jax.ShapeDtypeStruct(m.shape, BF16...  0.88 us
    convert_element_type x1, other arithmetic, per_device(): masked = increment * land_sea.astype(increment.dtype)[:, :, None]  0.68 us
    ppermute x1, starting transfers between devices, per_device(): z_other = lax.ppermute(z, 'comp', [(0, 1), (1, 0)])  0.52 us
  transfers between devices with their start and end apart: 1, of which 1 were waited for; matrix products, arithmetic and copies ran while one was open for 0% of the time, Pallas kernels for 0%

profile of v6, /device:TPU:0, one launch (start us, length us, event | category | flops | bytes accessed | tf_op | source)
XLA Modules:
  0.0 20.1 jit_solution(2643643890900268282)
XLA Ops:
  0.0 0.7 %convert_element_type.3 = bf16[4,128]{1,0:T(4,128)(2,1)S(1)} convert(s32[4,128]{1,0:T(4,128)} %sea_ref.1) | non-fusion elementwise | flops 512 | bytes 3072 | tf_op jit(solution)/shard_map/convert_element_type | solution.py:145
  0.7 0.0 copy-start.1
  0.7 1.0 %broadcast_multiply_fusion.m_ref = bf16[4,128,128]{2,1,0:T(8,128)(2,1)S(1)} fusion(bf16[4,128,128]{2,1,0:T(8,128)(2,1)} %param.5, bf16[4,128]{1,0:T(4,128)(2,1)S(1)} %convert_element_type.3), kind=kLoop, calls=%fused_computation | loop fusion | flops 65536 | bytes 263168 | tf_op jit(solution)/shard_map/mul | solution.py:145
  1.7 0.0 copy-done.1
  1.7 0.0 copy-start
  1.8 0.9 %shard_map.55.z_ref = bf16[4,128,128]{2,1,0:T(8,128)(2,1)S(1)} custom-call(bf16[4,128,128]{2,1,0:T(8,128)(2,1)S(1)} %broadcast_multiply_fusion.m_ref, f32[41,128]{1,0:T(8,128)S(1)} %copy-done.1), custom_call_target="tpu_custom_call" | custom-call | flops 5373952 | bytes 262144 | tf_op jit(solution)/shard_map/pallas_call | solution.py:47
  2.6 0.5 %collective-permute-start = (bf16[4,128,128]{2,1,0:T(8,128)(2,1)S(1)}, bf16[4,128,128]{2,1,0:T(8,128)(2,1)S(1)}, u32[]{:S(2)}, u32[]{:S(2)}) collective-permute-start(bf16[4,128,128]{2,1,0:T(8,128)(2,1)S(1)} %shard_map.55.z_ref), channel_id=1, source_target_pairs={{0,1},{1,0},{2,3},{3,2},{4,5},{5,4},{6,7},{7,6},{8,9},{9,8},{10,11... | collective-permute-start | bytes 393224 | tf_op jit(solution)/shard_map/ppermute | solution.py:147
  3.2 0.0 copy-start.3
  3.2 1.0 %collective-permute-done.zo_ref = bf16[4,128,128]{2,1,0:T(8,128)(2,1)S(1)} collective-permute-done((bf16[4,128,128]{2,1,0:T(8,128)(2,1)S(1)}, bf16[4,128,128]{2,1,0:T(8,128)(2,1)S(1)}, u32[]{:S(2)}, u32[]{:S(2)}) %collective-permute-start) | collective-permute-done | bytes 131104 | tf_op jit(solution)/shard_map/ppermute | solution.py:147
  4.1 0.0 copy-done
  4.2 0.0 copy-done.3
  4.2 0.3 %shard_map.56 = bf16[8,4,16,128]{3,2,1,0:T(8,128)(2,1)S(1)} custom-call(s32[1]{0:T(128)} %bitcast.c_ref, bf16[4,128,128]{2,1,0:T(8,128)(2,1)S(1)} %shard_map.55.z_ref, bf16[4,128,128]{2,1,0:T(8,128)(2,1)S(1)} %collective-permute-done.zo_ref, bf16[1,128,256]{2,1,0:T(8,128)(2,1)S(1)} %copy-done, s32[4,128]{1,0:T(4,128)S(1)} %copy-done.3), custom_call_target="tpu_custom_call" | custom-call | flops 33554432 | bytes 458752 | tf_op jit(solution)/shard_map/pallas_call | solution.py:81
  4.5 0.0 copy-start.2
  4.5 14.3 %all_to_all.5 = bf16[8,4,16,128]{3,2,1,0:T(8,128)(2,1)S(1)} all-to-all(bf16[8,4,16,128]{3,2,1,0:T(8,128)(2,1)S(1)} %shard_map.56), channel_id=1, replica_groups=mesh['ens'=2,'tile'=8,'comp'=2] {'tile'}, dimensions={0} | all-to-all | bytes 262144 | tf_op jit(solution)/shard_map/all_to_all | solution.py:150
  18.8 0.0 copy-done.2
  18.8 1.2 %shard_map.57 = bf16[32,16,128]{2,1,0:T(8,128)(2,1)} custom-call(bf16[32,16,128]{2,1,0:T(8,128)(2,1)S(1)} %bitcast.2, f32[41,128]{1,0:T(8,128)S(1)} %copy-done.2), custom_call_target="tpu_custom_call" | custom-call | flops 5373952 | bytes 262144 | tf_op jit(solution)/shard_map/pallas_call | solution.py:131
Async XLA Ops:
  0.7 1.1 %copy-start.1 = (f32[41,128]{1,0:T(8,128)S(1)}, f32[41,128]{1,0:T(8,128)}, u32[]{:S(2)}) copy-start(f32[41,128]{1,0:T(8,128)} %kx_ref.1) | copy-start | bytes 62980
  1.7 2.4 %copy-start = (bf16[1,128,256]{2,1,0:T(8,128)(2,1)S(1)}, bf16[1,128,256]{2,1,0:T(8,128)(2,1)}, u32[]{:S(2)}) copy-start(bf16[1,128,256]{2,1,0:T(8,128)(2,1)} %b_ref.1) | copy-start | bytes 196612
  2.6 1.5 %collective-permute-start = (bf16[4,128,128]{2,1,0:T(8,128)(2,1)S(1)}, bf16[4,128,128]{2,1,0:T(8,128)(2,1)S(1)}, u32[]{:S(2)}, u32[]{:S(2)}) collective-permute-start(bf16[4,128,128]{2,1,0:T(8,128)(2,1)S(1)} %shard_map.55.z_ref), channel_id=1, source_target_pairs={{0,1},{1,0},{2,3},{3,2},{4,5},{5,4},{6,7},{7,6},{8,9},{9,8},{10,11... | collective-permute-start | bytes 393224 | tf_op jit(solution)/shard_map/ppermute | solution.py:147
  3.2 1.0 %copy-start.3 = (s32[4,128]{1,0:T(4,128)S(1)}, s32[4,128]{1,0:T(4,128)}, u32[]{:S(2)}) copy-start(s32[4,128]{1,0:T(4,128)} %sea_ref.1) | copy-start | bytes 6148
  4.5 14.3 %copy-start.2 = (f32[41,128]{1,0:T(8,128)S(1)}, f32[41,128]{1,0:T(8,128)}, u32[]{:S(2)}) copy-start(f32[41,128]{1,0:T(8,128)} %ky_ref.1) | copy-start | bytes 62980

commit v7 on v6

--- a/solution.py
+++ b/solution.py
@@ -97,31 +97,36 @@
     ny, w, ch = m_ref.shape
     taps = ky_ref.shape[0]
     half = (taps - 1) // 2
+    chunk = min(ny, 8)
+    n_chunks = ny // chunk
+    if n_chunks <= 8:
+        pad_ref[0:ny] = m_ref[...].astype(F32)
+        for c in range(n_chunks):
+            y0 = c * chunk
+            acc = [None] * chunk
+            for k in range(taps):
+                d = k - half
+                lo, hi = max(0, -d - y0), min(chunk, ny - d - y0)
+                if lo >= hi:
+                    continue
+                term = ky_ref[k : k + 1, :][None] * pad_ref[y0 + d + lo : y0 + d + hi]
+                for y in range(lo, hi):
+                    acc[y] = term[y - lo] if acc[y] is None else acc[y] + term[y - lo]
+            out_ref[y0 : y0 + chunk] = jnp.stack(acc).astype(out_ref.dtype)
+        return
     pad_ref[0:half] = jnp.zeros((half, w, ch), F32)
     pad_ref[half + ny :] = jnp.zeros((half, w, ch), F32)
     pad_ref[half : half + ny] = m_ref[...].astype(F32)
-    chunk = min(ny, 8)
-    n_chunks = ny // chunk
 
-    def rows_at(y0, lo, hi):
+    def body(i, carry):
+        y0 = pl.multiple_of(i * chunk, chunk)
         acc = jnp.zeros((chunk, w, ch), F32)
-        for k in range(lo, hi):
+        for k in range(taps):
             acc = acc + ky_ref[k : k + 1, :][None] * pad_ref[pl.ds(y0 + k, chunk)]
         out_ref[pl.ds(y0, chunk)] = acc.astype(out_ref.dtype)
+        return carry
 
-    if n_chunks <= 8:
-        for c in range(n_chunks):
-            y0 = c * chunk
-            lo = max(0, half - y0 - chunk + 1)
-            hi = min(taps, half + ny - y0)
-            rows_at(y0, lo, hi)
-    else:
-
-        def body(i, carry):
-            rows_at(pl.multiple_of(i * chunk, chunk), 0, taps)
-            return carry
-
-        lax.fori_loop(0, n_chunks, body, 0)
+    lax.fori_loop(0, n_chunks, body, 0)
 
 
 def meridional(m, ky):

time: 20.3 us -> 20.2 us (level)
  no operation moved by 1% of the time
where the time goes in v7:
time: 20.2 us; the launch traced here: 20 us
  blocking collectives  14.3 us (71%)
  Pallas kernels  2.37 us (12%)
  other arithmetic  1.72 us (9%)
  waiting for transfers between devices  0.98 us (5%)
  starting transfers between devices  0.52 us (3%)
    all_to_all x1, blocking collectives, per_device(): lax.all_to_all(mixed, 'tile', split_axis=0, concat_axis=0, tiled=True)  14.3 us
    pallas_call x1, Pallas kernels, meridional(): pl.pallas_call(meridional_kernel, out_shape=jax.ShapeDtypeStruct(m.shape,...  1.15 us
    mul x1, other arithmetic, per_device(): masked = increment * land_sea.astype(increment.dtype)[:, :, None]  1.04 us
    ppermute x1, waiting for transfers between devices, per_device(): z_other = lax.ppermute(z, 'comp', [(0, 1), (1, 0)])  0.98 us
    pallas_call x1, Pallas kernels, zonal(): pl.pallas_call(zonal_kernel, out_shape=jax.ShapeDtypeStruct(m.shape, BF16...  0.88 us
    convert_element_type x1, other arithmetic, per_device(): masked = increment * land_sea.astype(increment.dtype)[:, :, None]  0.68 us
    ppermute x1, starting transfers between devices, per_device(): z_other = lax.ppermute(z, 'comp', [(0, 1), (1, 0)])  0.52 us
  transfers between devices with their start and end apart: 1, of which 1 were waited for; matrix products, arithmetic and copies ran while one was open for 0% of the time, Pallas kernels for 0%

profile of v7, /device:TPU:0, one launch (start us, length us, event | category | flops | bytes accessed | tf_op | source)
XLA Modules:
  0.0 20.0 jit_solution(405288918098733181)
XLA Ops:
  0.0 0.7 %convert_element_type.3 = bf16[4,128]{1,0:T(4,128)(2,1)S(1)} convert(s32[4,128]{1,0:T(4,128)} %sea_ref.1) | non-fusion elementwise | flops 512 | bytes 3072 | tf_op jit(solution)/shard_map/convert_element_type | solution.py:150
  0.7 0.0 copy-start.1
  0.7 1.0 %broadcast_multiply_fusion.m_ref = bf16[4,128,128]{2,1,0:T(8,128)(2,1)S(1)} fusion(bf16[4,128,128]{2,1,0:T(8,128)(2,1)} %param.5, bf16[4,128]{1,0:T(4,128)(2,1)S(1)} %convert_element_type.3), kind=kLoop, calls=%fused_computation | loop fusion | flops 65536 | bytes 263168 | tf_op jit(solution)/shard_map/mul | solution.py:150
  1.7 0.0 copy-done.1
  1.7 0.0 copy-start
  1.8 0.9 %shard_map.55.z_ref = bf16[4,128,128]{2,1,0:T(8,128)(2,1)S(1)} custom-call(bf16[4,128,128]{2,1,0:T(8,128)(2,1)S(1)} %broadcast_multiply_fusion.m_ref, f32[41,128]{1,0:T(8,128)S(1)} %copy-done.1), custom_call_target="tpu_custom_call" | custom-call | flops 5373952 | bytes 262144 | tf_op jit(solution)/shard_map/pallas_call | solution.py:47
  2.6 0.5 %collective-permute-start = (bf16[4,128,128]{2,1,0:T(8,128)(2,1)S(1)}, bf16[4,128,128]{2,1,0:T(8,128)(2,1)S(1)}, u32[]{:S(2)}, u32[]{:S(2)}) collective-permute-start(bf16[4,128,128]{2,1,0:T(8,128)(2,1)S(1)} %shard_map.55.z_ref), channel_id=1, source_target_pairs={{0,1},{1,0},{2,3},{3,2},{4,5},{5,4},{6,7},{7,6},{8,9},{9,8},{10,11... | collective-permute-start | bytes 393224 | tf_op jit(solution)/shard_map/ppermute | solution.py:152
  3.2 0.0 copy-start.3
  3.2 1.0 %collective-permute-done.zo_ref = bf16[4,128,128]{2,1,0:T(8,128)(2,1)S(1)} collective-permute-done((bf16[4,128,128]{2,1,0:T(8,128)(2,1)S(1)}, bf16[4,128,128]{2,1,0:T(8,128)(2,1)S(1)}, u32[]{:S(2)}, u32[]{:S(2)}) %collective-permute-start) | collective-permute-done | bytes 131104 | tf_op jit(solution)/shard_map/ppermute | solution.py:152
  4.1 0.0 copy-done
  4.2 0.0 copy-done.3
  4.2 0.3 %shard_map.56 = bf16[8,4,16,128]{3,2,1,0:T(8,128)(2,1)S(1)} custom-call(s32[1]{0:T(128)} %bitcast.c_ref, bf16[4,128,128]{2,1,0:T(8,128)(2,1)S(1)} %shard_map.55.z_ref, bf16[4,128,128]{2,1,0:T(8,128)(2,1)S(1)} %collective-permute-done.zo_ref, bf16[1,128,256]{2,1,0:T(8,128)(2,1)S(1)} %copy-done, s32[4,128]{1,0:T(4,128)S(1)} %copy-done.3), custom_call_target="tpu_custom_call" | custom-call | flops 33554432 | bytes 458752 | tf_op jit(solution)/shard_map/pallas_call | solution.py:81
  4.5 0.0 copy-start.2
  4.5 14.3 %all_to_all.5 = bf16[8,4,16,128]{3,2,1,0:T(8,128)(2,1)S(1)} all-to-all(bf16[8,4,16,128]{3,2,1,0:T(8,128)(2,1)S(1)} %shard_map.56), channel_id=1, replica_groups=mesh['ens'=2,'tile'=8,'comp'=2] {'tile'}, dimensions={0} | all-to-all | bytes 262144 | tf_op jit(solution)/shard_map/all_to_all | solution.py:155
  18.8 0.0 copy-done.2
  18.8 1.2 %shard_map.57 = bf16[32,16,128]{2,1,0:T(8,128)(2,1)} custom-call(bf16[32,16,128]{2,1,0:T(8,128)(2,1)S(1)} %bitcast.2, f32[41,128]{1,0:T(8,128)S(1)} %copy-done.2), custom_call_target="tpu_custom_call" | custom-call | flops 5373952 | bytes 262144 | tf_op jit(solution)/shard_map/pallas_call | solution.py:136
Async XLA Ops:
  0.7 1.1 %copy-start.1 = (f32[41,128]{1,0:T(8,128)S(1)}, f32[41,128]{1,0:T(8,128)}, u32[]{:S(2)}) copy-start(f32[41,128]{1,0:T(8,128)} %kx_ref.1) | copy-start | bytes 62980
  1.7 2.4 %copy-start = (bf16[1,128,256]{2,1,0:T(8,128)(2,1)S(1)}, bf16[1,128,256]{2,1,0:T(8,128)(2,1)}, u32[]{:S(2)}) copy-start(bf16[1,128,256]{2,1,0:T(8,128)(2,1)} %b_ref.1) | copy-start | bytes 196612
  2.6 1.5 %collective-permute-start = (bf16[4,128,128]{2,1,0:T(8,128)(2,1)S(1)}, bf16[4,128,128]{2,1,0:T(8,128)(2,1)S(1)}, u32[]{:S(2)}, u32[]{:S(2)}) collective-permute-start(bf16[4,128,128]{2,1,0:T(8,128)(2,1)S(1)} %shard_map.55.z_ref), channel_id=1, source_target_pairs={{0,1},{1,0},{2,3},{3,2},{4,5},{5,4},{6,7},{7,6},{8,9},{9,8},{10,11... | collective-permute-start | bytes 393224 | tf_op jit(solution)/shard_map/ppermute | solution.py:152
  3.2 1.0 %copy-start.3 = (s32[4,128]{1,0:T(4,128)S(1)}, s32[4,128]{1,0:T(4,128)}, u32[]{:S(2)}) copy-start(s32[4,128]{1,0:T(4,128)} %sea_ref.1) | copy-start | bytes 6148
  4.5 14.3 %copy-start.2 = (f32[41,128]{1,0:T(8,128)S(1)}, f32[41,128]{1,0:T(8,128)}, u32[]{:S(2)}) copy-start(f32[41,128]{1,0:T(8,128)} %ky_ref.1) | copy-start | bytes 62980

commit v8 on v7

--- a/solution.py
+++ b/solution.py
@@ -93,7 +93,7 @@
     )(c, z, zo, b, sea)
 
 
-def meridional_kernel(m_ref, ky_ref, out_ref, pad_ref):
+def meridional_kernel(m_ref, ky_ref, out_hbm, pad_ref, res_ref, sems):
     ny, w, ch = m_ref.shape
     taps = ky_ref.shape[0]
     half = (taps - 1) // 2
@@ -101,6 +101,7 @@
     n_chunks = ny // chunk
     if n_chunks <= 8:
         pad_ref[0:ny] = m_ref[...].astype(F32)
+        copies = []
         for c in range(n_chunks):
             y0 = c * chunk
             acc = [None] * chunk
@@ -112,7 +113,12 @@
                 term = ky_ref[k : k + 1, :][None] * pad_ref[y0 + d + lo : y0 + d + hi]
                 for y in range(lo, hi):
                     acc[y] = term[y - lo] if acc[y] is None else acc[y] + term[y - lo]
-            out_ref[y0 : y0 + chunk] = jnp.stack(acc).astype(out_ref.dtype)
+            res_ref[y0 : y0 + chunk] = jnp.stack(acc).astype(res_ref.dtype)
+            copy = pltpu.make_async_copy(res_ref.at[y0 : y0 + chunk], out_hbm.at[y0 : y0 + chunk], sems.at[c])
+            copy.start()
+            copies.append(copy)
+        for copy in copies:
+            copy.wait()
         return
     pad_ref[0:half] = jnp.zeros((half, w, ch), F32)
     pad_ref[half + ny :] = jnp.zeros((half, w, ch), F32)
@@ -123,22 +129,30 @@
         acc = jnp.zeros((chunk, w, ch), F32)
         for k in range(taps):
             acc = acc + ky_ref[k : k + 1, :][None] * pad_ref[pl.ds(y0 + k, chunk)]
-        out_ref[pl.ds(y0, chunk)] = acc.astype(out_ref.dtype)
+        res_ref[pl.ds(y0, chunk)] = acc.astype(res_ref.dtype)
         return carry
 
     lax.fori_loop(0, n_chunks, body, 0)
+    copy = pltpu.make_async_copy(res_ref, out_hbm, sems.at[0])
+    copy.start()
+    copy.wait()
 
 
 def meridional(m, ky):
     ny, w, ch = m.shape
     taps = ky.shape[0]
     half = (taps - 1) // 2
+    n_chunks = ny // min(ny, 8)
     return pl.pallas_call(
         meridional_kernel,
         out_shape=jax.ShapeDtypeStruct(m.shape, BF16),
         in_specs=[VMEM_SPEC] * 2,
-        out_specs=VMEM_SPEC,
-        scratch_shapes=[pltpu.VMEM((ny + 2 * half, w, ch), F32)],
+        out_specs=pl.BlockSpec(memory_space=pl.ANY),
+        scratch_shapes=[
+            pltpu.VMEM((ny + 2 * half, w, ch), F32),
+            pltpu.VMEM(m.shape, BF16),
+            pltpu.SemaphoreType.DMA((n_chunks,)),
+        ],
         compiler_params=SMALL_VMEM,
         cost_estimate=pl.CostEstimate(
             flops=2 * taps * m.size, transcendentals=0, bytes_accessed=4 * m.size

time: 20.2 us -> 20.2 us (level)
  no operation moved by 1% of the time
where the time goes in v8:
time: 20.2 us; the launch traced here: 20 us
  blocking collectives  14.3 us (71%)
  Pallas kernels  2.36 us (12%)
  other arithmetic  1.72 us (9%)
  waiting for transfers between devices  0.98 us (5%)
  starting transfers between devices  0.52 us (3%)
    all_to_all x1, blocking collectives, per_device(): lax.all_to_all(mixed, 'tile', split_axis=0, concat_axis=0, tiled=True)  14.3 us
    pallas_call x1, Pallas kernels, meridional(): pl.pallas_call(meridional_kernel, out_shape=jax.ShapeDtypeStruct(m.shape,...  1.14 us
    mul x1, other arithmetic, per_device(): masked = increment * land_sea.astype(increment.dtype)[:, :, None]  1.04 us
    ppermute x1, waiting for transfers between devices, per_device(): z_other = lax.ppermute(z, 'comp', [(0, 1), (1, 0)])  0.98 us
    pallas_call x1, Pallas kernels, zonal(): pl.pallas_call(zonal_kernel, out_shape=jax.ShapeDtypeStruct(m.shape, BF16...  0.88 us
    convert_element_type x1, other arithmetic, per_device(): masked = increment * land_sea.astype(increment.dtype)[:, :, None]  0.68 us
    ppermute x1, starting transfers between devices, per_device(): z_other = lax.ppermute(z, 'comp', [(0, 1), (1, 0)])  0.52 us
  transfers between devices with their start and end apart: 1, of which 1 were waited for; matrix products, arithmetic and copies ran while one was open for 0% of the time, Pallas kernels for 0%

profile of v8, /device:TPU:0, one launch (start us, length us, event | category | flops | bytes accessed | tf_op | source)
XLA Modules:
  0.0 20.0 jit_solution(6776775568254283742)
XLA Ops:
  0.0 0.7 %convert_element_type.3 = bf16[4,128]{1,0:T(4,128)(2,1)S(1)} convert(s32[4,128]{1,0:T(4,128)} %sea_ref.1) | non-fusion elementwise | flops 512 | bytes 3072 | tf_op jit(solution)/shard_map/convert_element_type | solution.py:164
  0.7 0.0 copy-start.1
  0.7 1.0 %broadcast_multiply_fusion.m_ref = bf16[4,128,128]{2,1,0:T(8,128)(2,1)S(1)} fusion(bf16[4,128,128]{2,1,0:T(8,128)(2,1)} %param.5, bf16[4,128]{1,0:T(4,128)(2,1)S(1)} %convert_element_type.3), kind=kLoop, calls=%fused_computation | loop fusion | flops 65536 | bytes 263168 | tf_op jit(solution)/shard_map/mul | solution.py:164
  1.7 0.0 copy-done.1
  1.7 0.0 copy-start
  1.8 0.9 %shard_map.55.z_ref = bf16[4,128,128]{2,1,0:T(8,128)(2,1)S(1)} custom-call(bf16[4,128,128]{2,1,0:T(8,128)(2,1)S(1)} %broadcast_multiply_fusion.m_ref, f32[41,128]{1,0:T(8,128)S(1)} %copy-done.1), custom_call_target="tpu_custom_call" | custom-call | flops 5373952 | bytes 262144 | tf_op jit(solution)/shard_map/pallas_call | solution.py:47
  2.6 0.5 %collective-permute-start = (bf16[4,128,128]{2,1,0:T(8,128)(2,1)S(1)}, bf16[4,128,128]{2,1,0:T(8,128)(2,1)S(1)}, u32[]{:S(2)}, u32[]{:S(2)}) collective-permute-start(bf16[4,128,128]{2,1,0:T(8,128)(2,1)S(1)} %shard_map.55.z_ref), channel_id=1, source_target_pairs={{0,1},{1,0},{2,3},{3,2},{4,5},{5,4},{6,7},{7,6},{8,9},{9,8},{10,11... | collective-permute-start | bytes 393224 | tf_op jit(solution)/shard_map/ppermute | solution.py:166
  3.2 0.0 copy-start.3
  3.2 1.0 %collective-permute-done.zo_ref = bf16[4,128,128]{2,1,0:T(8,128)(2,1)S(1)} collective-permute-done((bf16[4,128,128]{2,1,0:T(8,128)(2,1)S(1)}, bf16[4,128,128]{2,1,0:T(8,128)(2,1)S(1)}, u32[]{:S(2)}, u32[]{:S(2)}) %collective-permute-start) | collective-permute-done | bytes 131104 | tf_op jit(solution)/shard_map/ppermute | solution.py:166
  4.1 0.0 copy-done
  4.2 0.0 copy-done.3
  4.2 0.3 %shard_map.56 = bf16[8,4,16,128]{3,2,1,0:T(8,128)(2,1)S(1)} custom-call(s32[1]{0:T(128)} %bitcast.c_ref, bf16[4,128,128]{2,1,0:T(8,128)(2,1)S(1)} %shard_map.55.z_ref, bf16[4,128,128]{2,1,0:T(8,128)(2,1)S(1)} %collective-permute-done.zo_ref, bf16[1,128,256]{2,1,0:T(8,128)(2,1)S(1)} %copy-done, s32[4,128]{1,0:T(4,128)S(1)} %copy-done.3), custom_call_target="tpu_custom_call" | custom-call | flops 33554432 | bytes 458752 | tf_op jit(solution)/shard_map/pallas_call | solution.py:81
  4.5 0.0 copy-start.2
  4.5 14.3 %all_to_all.5 = bf16[8,4,16,128]{3,2,1,0:T(8,128)(2,1)S(1)} all-to-all(bf16[8,4,16,128]{3,2,1,0:T(8,128)(2,1)S(1)} %shard_map.56), channel_id=1, replica_groups=mesh['ens'=2,'tile'=8,'comp'=2] {'tile'}, dimensions={0} | all-to-all | bytes 262144 | tf_op jit(solution)/shard_map/all_to_all | solution.py:169
  18.8 0.0 copy-done.2
  18.8 1.1 %shard_map.57 = bf16[32,16,128]{2,1,0:T(8,128)(2,1)} custom-call(bf16[32,16,128]{2,1,0:T(8,128)(2,1)S(1)} %bitcast.2, f32[41,128]{1,0:T(8,128)S(1)} %copy-done.2), custom_call_target="tpu_custom_call" | custom-call | flops 5373952 | bytes 262144 | tf_op jit(solution)/shard_map/pallas_call | solution.py:146
Async XLA Ops:
  0.7 1.1 %copy-start.1 = (f32[41,128]{1,0:T(8,128)S(1)}, f32[41,128]{1,0:T(8,128)}, u32[]{:S(2)}) copy-start(f32[41,128]{1,0:T(8,128)} %kx_ref.1) | copy-start | bytes 62980
  1.7 2.4 %copy-start = (bf16[1,128,256]{2,1,0:T(8,128)(2,1)S(1)}, bf16[1,128,256]{2,1,0:T(8,128)(2,1)}, u32[]{:S(2)}) copy-start(bf16[1,128,256]{2,1,0:T(8,128)(2,1)} %b_ref.1) | copy-start | bytes 196612
  2.6 1.5 %collective-permute-start = (bf16[4,128,128]{2,1,0:T(8,128)(2,1)S(1)}, bf16[4,128,128]{2,1,0:T(8,128)(2,1)S(1)}, u32[]{:S(2)}, u32[]{:S(2)}) collective-permute-start(bf16[4,128,128]{2,1,0:T(8,128)(2,1)S(1)} %shard_map.55.z_ref), channel_id=1, source_target_pairs={{0,1},{1,0},{2,3},{3,2},{4,5},{5,4},{6,7},{7,6},{8,9},{9,8},{10,11... | collective-permute-start | bytes 393224 | tf_op jit(solution)/shard_map/ppermute | solution.py:166
  3.2 1.0 %copy-start.3 = (s32[4,128]{1,0:T(4,128)S(1)}, s32[4,128]{1,0:T(4,128)}, u32[]{:S(2)}) copy-start(s32[4,128]{1,0:T(4,128)} %sea_ref.1) | copy-start | bytes 6148
  4.5 14.3 %copy-start.2 = (f32[41,128]{1,0:T(8,128)S(1)}, f32[41,128]{1,0:T(8,128)}, u32[]{:S(2)}) copy-start(f32[41,128]{1,0:T(8,128)} %ky_ref.1) | copy-start | bytes 62980

commit v9 on v7

--- a/solution.py
+++ b/solution.py
@@ -57,19 +57,25 @@
     )(m, kx)
 
 
-def balance_kernel(c_ref, z_ref, zo_ref, b_ref, sea_ref, out_ref, seat_ref):
+def own_half_kernel(c_ref, z_ref, b_ref, out_ref):
+    rows, _, ch = z_ref.shape
+    c = c_ref[0]
+    own = b_ref[0, :, pl.ds(pl.multiple_of(c * ch, ch), ch)]
+    for r in range(rows):
+        out_ref[r] = lax.dot_general(z_ref[r], own, (((1,), (1,)), ((), ())), preferred_element_type=F32)
+
+
+def balance_kernel(c_ref, p_ref, zo_ref, b_ref, sea_ref, out_ref, seat_ref):
     nt, rows, width, _ = out_ref.shape
-    nx, ch = z_ref.shape[1], z_ref.shape[2]
+    nx, ch = zo_ref.shape[1], zo_ref.shape[2]
     sea = sea_ref[...].astype(F32)
     sea_pad = jnp.concatenate([sea, jnp.zeros((128 - rows, nx), F32)], axis=0)
     seat_ref[...] = jnp.transpose(sea_pad)
     c = c_ref[0]
-    own = b_ref[0, :, pl.ds(pl.multiple_of(c * ch, ch), ch)]
     other = b_ref[0, :, pl.ds(pl.multiple_of((1 - c) * ch, ch), ch)]
     dims = (((1,), (1,)), ((), ()))
     for r in range(rows):
-        res = lax.dot_general(z_ref[r], own, dims, preferred_element_type=F32)
-        res = res + lax.dot_general(zo_ref[r], other, dims, preferred_element_type=F32)
+        res = p_ref[r] + lax.dot_general(zo_ref[r], other, dims, preferred_element_type=F32)
         res = (res * seat_ref[:, r : r + 1]).astype(out_ref.dtype)
         for t in range(nt):
             out_ref[t, r] = res[t * width : (t + 1) * width]
@@ -78,19 +84,32 @@
 def balance_mix(c, z, zo, b, sea, nt):
     rows, nx, ch = z.shape
     ci = b.shape[1]
+    smem = pl.BlockSpec(memory_space=pltpu.SMEM)
+    partial = pl.pallas_call(
+        own_half_kernel,
+        out_shape=jax.ShapeDtypeStruct((rows, nx, ci), F32),
+        in_specs=[smem] + [VMEM_SPEC] * 2,
+        out_specs=VMEM_SPEC,
+        compiler_params=SMALL_VMEM,
+        cost_estimate=pl.CostEstimate(
+            flops=2 * rows * nx * ch * ci,
+            transcendentals=0,
+            bytes_accessed=2 * (z.size + b.size) + 4 * rows * nx * ci,
+        ),
+    )(c, z, b)
     return pl.pallas_call(
         balance_kernel,
         out_shape=jax.ShapeDtypeStruct((nt, rows, nx // nt, ci), BF16),
-        in_specs=[pl.BlockSpec(memory_space=pltpu.SMEM)] + [VMEM_SPEC] * 4,
+        in_specs=[smem] + [VMEM_SPEC] * 4,
         out_specs=VMEM_SPEC,
         scratch_shapes=[pltpu.VMEM((nx, 128), F32)],
         compiler_params=SMALL_VMEM,
         cost_estimate=pl.CostEstimate(
-            flops=4 * rows * nx * ch * ci,
+            flops=2 * rows * nx * ch * ci,
             transcendentals=0,
-            bytes_accessed=2 * (2 * z.size + b.size + rows * nx * ci),
+            bytes_accessed=2 * (zo.size + b.size + rows * nx * ci) + 4 * rows * nx * ci,
         ),
-    )(c, z, zo, b, sea)
+    )(c, partial, zo, b, sea)
 
 
 def meridional_kernel(m_ref, ky_ref, out_ref, pad_ref):

time: 20.2 us -> 20.2 us (level)
  Pallas kernels: 2.37 us -> 2.59 us
  waiting for transfers between devices: 0.98 us -> 0.77 us
    ppermute x1, waiting for transfers between devices: 0.98 us -> 0.77 us  [per_device(): z_other = lax.ppermute(z, 'comp', [(0, 1), (1, 0)])]
    pallas_call x0 -> x1, Pallas kernels: none -> 0.21 us  [balance_mix(): pl.pallas_call(own_half_kernel, out_shape=jax.ShapeDtypeStruct((rows, nx,...]
  transfers between devices with their start and end apart: 1 -> 1, of which waited for: 1 -> 1; matrix products, arithmetic and copies ran while one was open for 0% -> 0% of each run, Pallas kernels for 0% -> 1%
where the time goes in v9:
time: 20.2 us; the launch traced here: 20 us
  blocking collectives  14.3 us (71%)
  Pallas kernels  2.59 us (13%)
  other arithmetic  1.72 us (9%)
  waiting for transfers between devices  0.77 us (4%)
  starting transfers between devices  0.52 us (3%)
    all_to_all x1, blocking collectives, per_device(): lax.all_to_all(mixed, 'tile', split_axis=0, concat_axis=0, tiled=True)  14.3 us
    pallas_call x1, Pallas kernels, meridional(): pl.pallas_call(meridional_kernel, out_shape=jax.ShapeDtypeStruct(m.shape,...  1.15 us
    mul x1, other arithmetic, per_device(): masked = increment * land_sea.astype(increment.dtype)[:, :, None]  1.04 us
    pallas_call x1, Pallas kernels, zonal(): pl.pallas_call(zonal_kernel, out_shape=jax.ShapeDtypeStruct(m.shape, BF16...  0.93 us
    ppermute x1, waiting for transfers between devices, per_device(): z_other = lax.ppermute(z, 'comp', [(0, 1), (1, 0)])  0.77 us
    convert_element_type x1, other arithmetic, per_device(): masked = increment * land_sea.astype(increment.dtype)[:, :, None]  0.68 us
    ppermute x1, starting transfers between devices, per_device(): z_other = lax.ppermute(z, 'comp', [(0, 1), (1, 0)])  0.52 us
  transfers between devices with their start and end apart: 1, of which 1 were waited for; matrix products, arithmetic and copies ran while one was open for 0% of the time, Pallas kernels for 1%

profile of v9, /device:TPU:0, one launch (start us, length us, event | category | flops | bytes accessed | tf_op | source)
XLA Modules:
  0.0 20.0 jit_solution(13620956416195306463)
XLA Ops:
  0.0 0.7 %convert_element_type.3 = bf16[4,128]{1,0:T(4,128)(2,1)S(1)} convert(s32[4,128]{1,0:T(4,128)} %sea_ref.1) | non-fusion elementwise | flops 512 | bytes 3072 | tf_op jit(solution)/shard_map/convert_element_type | solution.py:169
  0.7 0.0 copy-start.1
  0.7 1.0 %broadcast_multiply_fusion.m_ref = bf16[4,128,128]{2,1,0:T(8,128)(2,1)S(1)} fusion(bf16[4,128,128]{2,1,0:T(8,128)(2,1)} %param.5, bf16[4,128]{1,0:T(4,128)(2,1)S(1)} %convert_element_type.3), kind=kLoop, calls=%fused_computation | loop fusion | flops 65536 | bytes 263168 | tf_op jit(solution)/shard_map/mul | solution.py:169
  1.7 0.0 copy-done.1
  1.7 0.0 copy-start
  1.8 0.9 %shard_map.55.z_ref = bf16[4,128,128]{2,1,0:T(8,128)(2,1)S(1)} custom-call(bf16[4,128,128]{2,1,0:T(8,128)(2,1)S(1)} %broadcast_multiply_fusion.m_ref, f32[41,128]{1,0:T(8,128)S(1)} %copy-done.1), custom_call_target="tpu_custom_call" | custom-call | flops 5373952 | bytes 262144 | tf_op jit(solution)/shard_map/pallas_call | solution.py:47
  2.7 0.5 %collective-permute-start = (bf16[4,128,128]{2,1,0:T(8,128)(2,1)S(1)}, bf16[4,128,128]{2,1,0:T(8,128)(2,1)S(1)}, u32[]{:S(2)}, u32[]{:S(2)}) collective-permute-start(bf16[4,128,128]{2,1,0:T(8,128)(2,1)S(1)} %shard_map.55.z_ref), channel_id=1, source_target_pairs={{0,1},{1,0},{2,3},{3,2},{4,5},{5,4},{6,7},{7,6},{8,9},{9,8},{10,11... | collective-permute-start | bytes 393224 | tf_op jit(solution)/shard_map/ppermute | solution.py:171
  3.2 0.0 copy-done
  3.2 0.0 copy-start.3
  3.2 0.2 %shard_map.56.p_ref = f32[4,128,128]{2,1,0:T(8,128)S(1)} custom-call(s32[1]{0:T(128)} %bitcast.c_ref, bf16[4,128,128]{2,1,0:T(8,128)(2,1)S(1)} %shard_map.55.z_ref, bf16[1,128,256]{2,1,0:T(8,128)(2,1)S(1)} %copy-done), custom_call_target="tpu_custom_call" | custom-call | flops 16777216 | bytes 458752 | tf_op jit(solution)/shard_map/pallas_call | solution.py:88
  3.4 0.8 %collective-permute-done.zo_ref = bf16[4,128,128]{2,1,0:T(8,128)(2,1)S(1)} collective-permute-done((bf16[4,128,128]{2,1,0:T(8,128)(2,1)S(1)}, bf16[4,128,128]{2,1,0:T(8,128)(2,1)S(1)}, u32[]{:S(2)}, u32[]{:S(2)}) %collective-permute-start) | collective-permute-done | bytes 131104 | tf_op jit(solution)/shard_map/ppermute | solution.py:171
  4.2 0.0 copy-done.3
  4.2 0.3 %shard_map.57 = bf16[8,4,16,128]{3,2,1,0:T(8,128)(2,1)S(1)} custom-call(s32[1]{0:T(128)} %bitcast.c_ref, f32[4,128,128]{2,1,0:T(8,128)S(1)} %shard_map.56.p_ref, bf16[4,128,128]{2,1,0:T(8,128)(2,1)S(1)} %collective-permute-done.zo_ref, bf16[1,128,256]{2,1,0:T(8,128)(2,1)S(1)} %copy-done, s32[4,128]{1,0:T(4,128)S(1)} %copy-done.3), custom_call_target="tpu_custom_call" | custom-call | flops 16777216 | bytes 589824 | tf_op jit(solution)/shard_map/pallas_call | solution.py:100
  4.5 0.0 copy-start.2
  4.5 14.3 %all_to_all.5 = bf16[8,4,16,128]{3,2,1,0:T(8,128)(2,1)S(1)} all-to-all(bf16[8,4,16,128]{3,2,1,0:T(8,128)(2,1)S(1)} %shard_map.57), channel_id=1, replica_groups=mesh['ens'=2,'tile'=8,'comp'=2] {'tile'}, dimensions={0} | all-to-all | bytes 262144 | tf_op jit(solution)/shard_map/all_to_all | solution.py:174
  18.8 0.0 copy-done.2
  18.9 1.2 %shard_map.58 = bf16[32,16,128]{2,1,0:T(8,128)(2,1)} custom-call(bf16[32,16,128]{2,1,0:T(8,128)(2,1)S(1)} %bitcast.2, f32[41,128]{1,0:T(8,128)S(1)} %copy-done.2), custom_call_target="tpu_custom_call" | custom-call | flops 5373952 | bytes 262144 | tf_op jit(solution)/shard_map/pallas_call | solution.py:155
Async XLA Ops:
  0.7 1.1 %copy-start.1 = (f32[41,128]{1,0:T(8,128)S(1)}, f32[41,128]{1,0:T(8,128)}, u32[]{:S(2)}) copy-start(f32[41,128]{1,0:T(8,128)} %kx_ref.1) | copy-start | bytes 62980
  1.7 1.5 %copy-start = (bf16[1,128,256]{2,1,0:T(8,128)(2,1)S(1)}, bf16[1,128,256]{2,1,0:T(8,128)(2,1)}, u32[]{:S(2)}) copy-start(bf16[1,128,256]{2,1,0:T(8,128)(2,1)} %b_ref.3) | copy-start | bytes 196612
  2.7 1.5 %collective-permute-start = (bf16[4,128,128]{2,1,0:T(8,128)(2,1)S(1)}, bf16[4,128,128]{2,1,0:T(8,128)(2,1)S(1)}, u32[]{:S(2)}, u32[]{:S(2)}) collective-permute-start(bf16[4,128,128]{2,1,0:T(8,128)(2,1)S(1)} %shard_map.55.z_ref), channel_id=1, source_target_pairs={{0,1},{1,0},{2,3},{3,2},{4,5},{5,4},{6,7},{7,6},{8,9},{9,8},{10,11... | collective-permute-start | bytes 393224 | tf_op jit(solution)/shard_map/ppermute | solution.py:171
  3.2 1.0 %copy-start.3 = (s32[4,128]{1,0:T(4,128)S(1)}, s32[4,128]{1,0:T(4,128)}, u32[]{:S(2)}) copy-start(s32[4,128]{1,0:T(4,128)} %sea_ref.1) | copy-start | bytes 6148
  4.5 14.3 %copy-start.2 = (f32[41,128]{1,0:T(8,128)S(1)}, f32[41,128]{1,0:T(8,128)}, u32[]{:S(2)}) copy-start(f32[41,128]{1,0:T(8,128)} %ky_ref.1) | copy-start | bytes 62980

commit v10 on v6

--- a/solution.py
+++ b/solution.py
@@ -13,15 +13,14 @@
 BF16 = jnp.bfloat16
 
 
-def zonal_kernel(m_ref, kx_ref, out_ref, ext_ref):
-    rows, nx, ch = m_ref.shape
+def zonal_rows(m_of, kx_ref, store, ext_ref, rows, nx, ch):
     taps = kx_ref.shape[0]
     half = (taps - 1) // 2
     pad = ((half + 7) // 8) * 8
     span = nx + 2 * pad - 8
     chunk = min(nx, 64)
     for r in range(rows):
-        m = m_ref[r].astype(F32)
+        m = m_of(r)
         ext = jnp.concatenate([m[nx - pad :], m, m[:pad]], axis=0)
         for s in range(8):
             ext_ref[s] = ext[s : s + span]
@@ -33,23 +32,36 @@
                 e = k - half + pad
                 q, s = divmod(e, 8)
                 acc = acc + kx_ref[k : k + 1, :] * ext_ref[s, pl.ds(x0 + 8 * q, chunk), :]
-            out_ref[r, pl.ds(x0, chunk), :] = acc.astype(out_ref.dtype)
+            store(r, x0, chunk, acc)
             return carry
 
         n_chunks = nx // chunk
         lax.fori_loop(0, n_chunks, body, 0, unroll=n_chunks <= 4)
 
 
+def ext_shape(nx, ch, taps):
+    pad = (((taps - 1) // 2 + 7) // 8) * 8
+    return (8, nx + 2 * pad - 8, ch)
+
+
+def zonal_kernel(m_ref, kx_ref, out_ref, ext_ref):
+    rows, nx, ch = m_ref.shape
+
+    def store(r, x0, chunk, acc):
+        out_ref[r, pl.ds(x0, chunk), :] = acc.astype(out_ref.dtype)
+
+    zonal_rows(lambda r: m_ref[r].astype(F32), kx_ref, store, ext_ref, rows, nx, ch)
+
+
 def zonal(m, kx):
     rows, nx, ch = m.shape
     taps = kx.shape[0]
-    pad = (((taps - 1) // 2 + 7) // 8) * 8
     return pl.pallas_call(
         zonal_kernel,
         out_shape=jax.ShapeDtypeStruct(m.shape, BF16),
         in_specs=[VMEM_SPEC] * 2,
         out_specs=VMEM_SPEC,
-        scratch_shapes=[pltpu.VMEM((8, nx + 2 * pad - 8, ch), F32)],
+        scratch_shapes=[pltpu.VMEM(ext_shape(nx, ch, taps), F32)],
         compiler_params=SMALL_VMEM,
         cost_estimate=pl.CostEstimate(
             flops=2 * taps * m.size, transcendentals=0, bytes_accessed=4 * m.size
@@ -57,12 +69,19 @@
     )(m, kx)
 
 
-def balance_kernel(c_ref, z_ref, zo_ref, b_ref, sea_ref, out_ref, seat_ref):
+def balance_kernel(c_ref, z_ref, io_ref, kxo_ref, b_ref, sea_ref, out_ref, zo_ref, ext_ref, seat_ref):
     nt, rows, width, _ = out_ref.shape
     nx, ch = z_ref.shape[1], z_ref.shape[2]
     sea = sea_ref[...].astype(F32)
     sea_pad = jnp.concatenate([sea, jnp.zeros((128 - rows, nx), F32)], axis=0)
     seat_ref[...] = jnp.transpose(sea_pad)
+
+    def store(r, x0, chunk, acc):
+        zo_ref[r, pl.ds(x0, chunk), :] = acc.astype(zo_ref.dtype)
+
+    zonal_rows(
+        lambda r: io_ref[r].astype(F32) * seat_ref[:, r : r + 1], kxo_ref, store, ext_ref, rows, nx, ch
+    )
     c = c_ref[0]
     own = b_ref[0, :, pl.ds(pl.multiple_of(c * ch, ch), ch)]
     other = b_ref[0, :, pl.ds(pl.multiple_of((1 - c) * ch, ch), ch)]
@@ -75,22 +94,27 @@
             out_ref[t, r] = res[t * width : (t + 1) * width]
 
 
-def balance_mix(c, z, zo, b, sea, nt):
+def balance_mix(c, z, io, kxo, b, sea, nt):
     rows, nx, ch = z.shape
     ci = b.shape[1]
+    taps = kxo.shape[0]
     return pl.pallas_call(
         balance_kernel,
         out_shape=jax.ShapeDtypeStruct((nt, rows, nx // nt, ci), BF16),
-        in_specs=[pl.BlockSpec(memory_space=pltpu.SMEM)] + [VMEM_SPEC] * 4,
+        in_specs=[pl.BlockSpec(memory_space=pltpu.SMEM)] + [VMEM_SPEC] * 5,
         out_specs=VMEM_SPEC,
-        scratch_shapes=[pltpu.VMEM((nx, 128), F32)],
+        scratch_shapes=[
+            pltpu.VMEM(z.shape, BF16),
+            pltpu.VMEM(ext_shape(nx, ch, taps), F32),
+            pltpu.VMEM((nx, 128), F32),
+        ],
         compiler_params=SMALL_VMEM,
         cost_estimate=pl.CostEstimate(
-            flops=4 * rows * nx * ch * ci,
+            flops=4 * rows * nx * ch * ci + 2 * taps * z.size,
             transcendentals=0,
             bytes_accessed=2 * (2 * z.size + b.size + rows * nx * ci),
         ),
-    )(c, z, zo, b, sea)
+    )(c, z, io, kxo, b, sea)
 
 
 def meridional_kernel(m_ref, ky_ref, out_ref, pad_ref):
@@ -142,11 +166,11 @@
 
 
 def per_device(nt, increment, land_sea, kernel_x, kernel_y, balance):
+    inc_other, kx_other = lax.ppermute((increment, kernel_x), "comp", [(0, 1), (1, 0)])
     masked = increment * land_sea.astype(increment.dtype)[:, :, None]
     z = zonal(masked, kernel_x)
-    z_other = lax.ppermute(z, "comp", [(0, 1), (1, 0)])
     c = lax.axis_index("comp").astype(jnp.int32).reshape(1)
-    mixed = balance_mix(c, z, z_other, balance, land_sea, nt)
+    mixed = balance_mix(c, z, inc_other, kx_other, balance, land_sea, nt)
     moved = lax.all_to_all(mixed, "tile", split_axis=0, concat_axis=0, tiled=True)
     nt_, rows, width, ch = moved.shape
     return meridional(moved.reshape(nt_ * rows, width, ch), kernel_y)

time: 20.3 us -> 20.4 us (level)
  Pallas kernels: 2.43 us -> 3.43 us
  waiting for transfers between devices: 0.98 us -> 0.01 us
    ppermute x1 -> x2, waiting for transfers between devices: 0.98 us -> 0.01 us  [per_device(): lax.ppermute((increment, kernel_x), 'comp', [(0, 1), (1, 0)])]
    pallas_call x1, Pallas kernels: 0.33 us -> 1.28 us  [balance_mix(): pl.pallas_call(balance_kernel, out_shape=jax.ShapeDtypeStruct((nt, rows,...]
    ppermute x1 -> x2, starting transfers between devices: 0.52 us -> 0.51 us  [per_device(): lax.ppermute((increment, kernel_x), 'comp', [(0, 1), (1, 0)])]
  transfers between devices with their start and end apart: 1 -> 2, of which waited for: 1 -> 0; matrix products, arithmetic and copies ran while one was open for 0% -> 9% of each run, Pallas kernels for 0% -> 5%
where the time goes in v10:
time: 20.4 us; the launch traced here: 20.2 us
  blocking collectives  14.4 us (71%)
  Pallas kernels  3.43 us (17%)
  other arithmetic  1.72 us (8%)
  starting transfers between devices  0.51 us (2%)
    all_to_all x1, blocking collectives, per_device(): lax.all_to_all(mixed, 'tile', split_axis=0, concat_axis=0, tiled=True)  14.4 us
    pallas_call x1, Pallas kernels, balance_mix(): pl.pallas_call(balance_kernel, out_shape=jax.ShapeDtypeStruct((nt, rows,...  1.28 us
    pallas_call x1, Pallas kernels, meridional(): pl.pallas_call(meridional_kernel, out_shape=jax.ShapeDtypeStruct(m.shape,...  1.22 us
    mul x1, other arithmetic, per_device(): masked = increment * land_sea.astype(increment.dtype)[:, :, None]  1.04 us
    pallas_call x1, Pallas kernels, zonal(): pl.pallas_call(zonal_kernel, out_shape=jax.ShapeDtypeStruct(m.shape, BF16...  0.92 us
    convert_element_type x1, other arithmetic, per_device(): masked = increment * land_sea.astype(increment.dtype)[:, :, None]  0.68 us
    ppermute x2, starting transfers between devices, per_device(): lax.ppermute((increment, kernel_x), 'comp', [(0, 1), (1, 0)])  0.51 us
  transfers between devices with their start and end apart: 2, of which 0 were waited for; matrix products, arithmetic and copies ran while one was open for 9% of the time, Pallas kernels for 5%

profile of v10, /device:TPU:0, one launch (start us, length us, event | category | flops | bytes accessed | tf_op | source)
XLA Modules:
  0.0 20.2 jit_solution(15434785000480507207)
XLA Ops:
  0.0 0.5 %collective-permute-start.1 = (f32[41,128]{1,0:T(8,128)}, f32[41,128]{1,0:T(8,128)S(1)}, u32[]{:S(2)}, u32[]{:S(2)}) collective-permute-start(f32[41,128]{1,0:T(8,128)} %kx_ref.1), channel_id=1, source_target_pairs={{0,1},{1,0},{2,3},{3,2},{4,5},{5,4},{6,7},{7,6},{8,9},{9,8},{10,11... | collective-permute-start | bytes 62984 | tf_op jit(solution)/shard_map/ppermute | solution.py:169
  0.5 0.1 collective-permute-start
  0.5 0.7 %convert_element_type.3 = bf16[4,128]{1,0:T(4,128)(2,1)S(1)} convert(s32[4,128]{1,0:T(4,128)} %sea_ref.1) | non-fusion elementwise | flops 512 | bytes 3072 | tf_op jit(solution)/shard_map/convert_element_type | solution.py:170
  1.2 0.0 copy-start.1
  1.2 1.0 %broadcast_multiply_fusion.m_ref = bf16[4,128,128]{2,1,0:T(8,128)(2,1)S(1)} fusion(bf16[4,128,128]{2,1,0:T(8,128)(2,1)} %param.5, bf16[4,128]{1,0:T(4,128)(2,1)S(1)} %convert_element_type.3), kind=kLoop, calls=%fused_computation | loop fusion | flops 65536 | bytes 263168 | tf_op jit(solution)/shard_map/mul | solution.py:170
  2.2 0.0 copy-done.1
  2.3 0.0 copy-start
  2.3 0.0 copy-start.3
  2.3 0.9 %shard_map.55.z_ref = bf16[4,128,128]{2,1,0:T(8,128)(2,1)S(1)} custom-call(bf16[4,128,128]{2,1,0:T(8,128)(2,1)S(1)} %broadcast_multiply_fusion.m_ref, f32[41,128]{1,0:T(8,128)S(1)} %copy-done.1), custom_call_target="tpu_custom_call" | custom-call | flops 5373952 | bytes 262144 | tf_op jit(solution)/shard_map/pallas_call | solution.py:59
  3.2 0.0 collective-permute-done.1.kxo_ref
  3.2 0.0 collective-permute-done.io_ref
  3.2 0.0 copy-done
  3.2 0.0 copy-done.3
  3.3 1.3 %shard_map.56 = bf16[8,4,16,128]{3,2,1,0:T(8,128)(2,1)S(1)} custom-call(s32[1]{0:T(128)} %bitcast.c_ref, bf16[4,128,128]{2,1,0:T(8,128)(2,1)S(1)} %shard_map.55.z_ref, bf16[4,128,128]{2,1,0:T(8,128)(2,1)S(1)} %collective-permute-done.io_ref, f32[41,128]{1,0:T(8,128)S(1)} %collective-permute-done.1.kxo_ref, bf16[1,128,256]{2,1,0:T(8,128)(2,1)S(1)} %copy-done, ...), custom_call_target="tpu_custom_call" | custom-call | flops 38928384 | bytes 458752 | tf_op jit(solution)/shard_map/pallas_call | solution.py:101
  4.5 0.0 copy-start.2
  4.6 14.4 %all_to_all.5 = bf16[8,4,16,128]{3,2,1,0:T(8,128)(2,1)S(1)} all-to-all(bf16[8,4,16,128]{3,2,1,0:T(8,128)(2,1)S(1)} %shard_map.56), channel_id=1, replica_groups=mesh['ens'=2,'tile'=8,'comp'=2] {'tile'}, dimensions={0} | all-to-all | bytes 262144 | tf_op jit(solution)/shard_map/all_to_all | solution.py:174
  19.0 0.0 copy-done.2
  19.0 1.2 %shard_map.57 = bf16[32,16,128]{2,1,0:T(8,128)(2,1)} custom-call(bf16[32,16,128]{2,1,0:T(8,128)(2,1)S(1)} %bitcast.2, f32[41,128]{1,0:T(8,128)S(1)} %copy-done.2), custom_call_target="tpu_custom_call" | custom-call | flops 5373952 | bytes 262144 | tf_op jit(solution)/shard_map/pallas_call | solution.py:155
Async XLA Ops:
  0.0 3.2 %collective-permute-start.1 = (f32[41,128]{1,0:T(8,128)}, f32[41,128]{1,0:T(8,128)S(1)}, u32[]{:S(2)}, u32[]{:S(2)}) collective-permute-start(f32[41,128]{1,0:T(8,128)} %kx_ref.1), channel_id=1, source_target_pairs={{0,1},{1,0},{2,3},{3,2},{4,5},{5,4},{6,7},{7,6},{8,9},{9,8},{10,11... | collective-permute-start | bytes 62984 | tf_op jit(solution)/shard_map/ppermute | solution.py:169
  0.5 2.8 %collective-permute-start = (bf16[4,128,128]{2,1,0:T(8,128)(2,1)}, bf16[4,128,128]{2,1,0:T(8,128)(2,1)S(1)}, u32[]{:S(2)}, u32[]{:S(2)}) collective-permute-start(bf16[4,128,128]{2,1,0:T(8,128)(2,1)} %param.5), channel_id=1, source_target_pairs={{0,1},{1,0},{2,3},{3,2},{4,5},{5,4},{6,7},{7,6},{8,9},{9,8},{10,11... | collective-permute-start | bytes 393224 | tf_op jit(solution)/shard_map/ppermute | solution.py:169
  1.2 1.1 %copy-start.1 = (f32[41,128]{1,0:T(8,128)S(1)}, f32[41,128]{1,0:T(8,128)}, u32[]{:S(2)}) copy-start(f32[41,128]{1,0:T(8,128)} %kx_ref.1) | copy-start | bytes 62980
  2.3 1.0 %copy-start = (bf16[1,128,256]{2,1,0:T(8,128)(2,1)S(1)}, bf16[1,128,256]{2,1,0:T(8,128)(2,1)}, u32[]{:S(2)}) copy-start(bf16[1,128,256]{2,1,0:T(8,128)(2,1)} %b_ref.1) | copy-start | bytes 196612
  2.3 1.0 %copy-start.3 = (s32[4,128]{1,0:T(4,128)S(1)}, s32[4,128]{1,0:T(4,128)}, u32[]{:S(2)}) copy-start(s32[4,128]{1,0:T(4,128)} %sea_ref.1) | copy-start | bytes 6148
  4.5 14.4 %copy-start.2 = (f32[41,128]{1,0:T(8,128)S(1)}, f32[41,128]{1,0:T(8,128)}, u32[]{:S(2)}) copy-start(f32[41,128]{1,0:T(8,128)} %ky_ref.1) | copy-start | bytes 62980

commit v11 on v6

--- a/solution.py
+++ b/solution.py
@@ -142,7 +142,10 @@
 
 
 def per_device(nt, increment, land_sea, kernel_x, kernel_y, balance):
-    masked = increment * land_sea.astype(increment.dtype)[:, :, None]
+    rows, nx, _ = increment.shape
+    on_diagonal = lax.broadcasted_iota(jnp.int32, (rows, nx, nx), 1) == lax.broadcasted_iota(jnp.int32, (rows, nx, nx), 2)
+    diag = jnp.where(on_diagonal, land_sea[:, :, None], 0).astype(increment.dtype)
+    masked = jnp.einsum("rxy,ryc->rxc", diag, increment, preferred_element_type=F32).astype(increment.dtype)
     z = zonal(masked, kernel_x)
     z_other = lax.ppermute(z, "comp", [(0, 1), (1, 0)])
     c = lax.axis_index("comp").astype(jnp.int32).reshape(1)

time: 20.3 us -> 20.4 us (level)
  other arithmetic: 1.72 us -> 0 us
  matrix products: 0 us -> 0.93 us
  local copies, waits for them, and re-layouts: 0.02 us -> 0.92 us
    mul x1 -> x0, other arithmetic: 1.04 us -> none  [per_device(): masked = increment * land_sea.astype(increment.dtype)[:, :, None]]
    dot_general x0 -> x1, matrix products: none -> 0.93 us  [per_device(): jnp.einsum('rxy,ryc->rxc', diag, increment, preferred_element_type=F32)]
    unnamed x8 -> x10, local copies, waits for them, and re-layouts: 0.02 us -> 0.92 us
    convert_element_type x1 -> x0, other arithmetic: 0.68 us -> none  [per_device(): masked = increment * land_sea.astype(increment.dtype)[:, :, None]]
where the time goes in v11:
time: 20.4 us; the launch traced here: 20.2 us
  blocking collectives  14.3 us (70%)
  Pallas kernels  2.43 us (12%)
  waiting for transfers between devices  0.98 us (5%)
  matrix products  0.93 us (5%)
  local copies, waits for them, and re-layouts  0.92 us (5%)
  starting transfers between devices  0.52 us (3%)
    all_to_all x1, blocking collectives, per_device(): lax.all_to_all(mixed, 'tile', split_axis=0, concat_axis=0, tiled=True)  14.3 us
    pallas_call x1, Pallas kernels, meridional(): pl.pallas_call(meridional_kernel, out_shape=jax.ShapeDtypeStruct(m.shape,...  1.22 us
    ppermute x1, waiting for transfers between devices, per_device(): z_other = lax.ppermute(z, 'comp', [(0, 1), (1, 0)])  0.98 us
    dot_general x1, matrix products, per_device(): jnp.einsum('rxy,ryc->rxc', diag, increment, preferred_element_type=F32)  0.93 us
    unnamed x10, local copies, waits for them, and re-layouts  0.92 us
    pallas_call x1, Pallas kernels, zonal(): pl.pallas_call(zonal_kernel, out_shape=jax.ShapeDtypeStruct(m.shape, BF16...  0.88 us
    ppermute x1, starting transfers between devices, per_device(): z_other = lax.ppermute(z, 'comp', [(0, 1), (1, 0)])  0.52 us
  transfers between devices with their start and end apart: 1, of which 1 were waited for; matrix products, arithmetic and copies ran while one was open for 0% of the time, Pallas kernels for 0%

profile of v11, /device:TPU:0, one launch (start us, length us, event | category | flops | bytes accessed | tf_op | source)
XLA Modules:
  0.0 20.2 jit_solution(3462388908561544376)
XLA Ops:
  0.0 0.0 copy-start
  0.0 0.0 copy-start.2
  0.0 0.9 %copy-done = bf16[4,128,128]{2,1,0:T(8,128)(2,1)S(1)} copy-done((bf16[4,128,128]{2,1,0:T(8,128)(2,1)S(1)}, bf16[4,128,128]{2,1,0:T(8,128)(2,1)}, u32[]{:S(2)}) %copy-start) | copy-done | bytes 131096
  0.9 0.9 %convolution_convert_fusion.m_ref = bf16[4,128,128]{2,1,0:T(8,128)(2,1)S(1)} fusion(bf16[4,128,128]{2,1,0:T(8,128)(2,1)S(1)} %copy-done, s32[4,128]{1,0:T(4,128)} %sea_ref.1), kind=kOutput, calls=%fused_computation | convolution fusion | flops 17039360 | bytes 264192 | tf_op jit(solution)/shard_map/rxy,ryc->rxc/dot_general | solution.py:148
  1.8 0.0 copy-done.2
  1.9 0.0 copy-start.1
  1.9 0.9 %shard_map.55.z_ref = bf16[4,128,128]{2,1,0:T(8,128)(2,1)S(1)} custom-call(bf16[4,128,128]{2,1,0:T(8,128)(2,1)S(1)} %convolution_convert_fusion.m_ref, f32[41,128]{1,0:T(8,128)S(1)} %copy-done.2), custom_call_target="tpu_custom_call" | custom-call | flops 5373952 | bytes 262144 | tf_op jit(solution)/shard_map/pallas_call | solution.py:47
  2.8 0.5 %collective-permute-start = (bf16[4,128,128]{2,1,0:T(8,128)(2,1)S(1)}, bf16[4,128,128]{2,1,0:T(8,128)(2,1)S(1)}, u32[]{:S(2)}, u32[]{:S(2)}) collective-permute-start(bf16[4,128,128]{2,1,0:T(8,128)(2,1)S(1)} %shard_map.55.z_ref), channel_id=1, source_target_pairs={{0,1},{1,0},{2,3},{3,2},{4,5},{5,4},{6,7},{7,6},{8,9},{9,8},{10,11... | collective-permute-start | bytes 393224 | tf_op jit(solution)/shard_map/ppermute | solution.py:150
  3.3 0.0 copy-start.4
  3.3 1.0 %collective-permute-done.zo_ref = bf16[4,128,128]{2,1,0:T(8,128)(2,1)S(1)} collective-permute-done((bf16[4,128,128]{2,1,0:T(8,128)(2,1)S(1)}, bf16[4,128,128]{2,1,0:T(8,128)(2,1)S(1)}, u32[]{:S(2)}, u32[]{:S(2)}) %collective-permute-start) | collective-permute-done | bytes 131104 | tf_op jit(solution)/shard_map/ppermute | solution.py:150
  4.3 0.0 copy-done.1
  4.3 0.0 copy-done.4
  4.3 0.3 %shard_map.56 = bf16[8,4,16,128]{3,2,1,0:T(8,128)(2,1)S(1)} custom-call(s32[1]{0:T(128)} %bitcast.c_ref, bf16[4,128,128]{2,1,0:T(8,128)(2,1)S(1)} %shard_map.55.z_ref, bf16[4,128,128]{2,1,0:T(8,128)(2,1)S(1)} %collective-permute-done.zo_ref, bf16[1,128,256]{2,1,0:T(8,128)(2,1)S(1)} %copy-done.1, s32[4,128]{1,0:T(4,128)S(1)} %copy-done.4), custom_call_target="tpu_custom_call" | custom-call | flops 33554432 | bytes 458752 | tf_op jit(solution)/shard_map/pallas_call | solution.py:81
  4.6 0.0 copy-start.3
  4.6 14.3 %all_to_all.5 = bf16[8,4,16,128]{3,2,1,0:T(8,128)(2,1)S(1)} all-to-all(bf16[8,4,16,128]{3,2,1,0:T(8,128)(2,1)S(1)} %shard_map.56), channel_id=1, replica_groups=mesh['ens'=2,'tile'=8,'comp'=2] {'tile'}, dimensions={0} | all-to-all | bytes 262144 | tf_op jit(solution)/shard_map/all_to_all | solution.py:153
  18.9 0.0 copy-done.3
  19.0 1.2 %shard_map.57 = bf16[32,16,128]{2,1,0:T(8,128)(2,1)} custom-call(bf16[32,16,128]{2,1,0:T(8,128)(2,1)S(1)} %bitcast.3, f32[41,128]{1,0:T(8,128)S(1)} %copy-done.3), custom_call_target="tpu_custom_call" | custom-call | flops 5373952 | bytes 262144 | tf_op jit(solution)/shard_map/pallas_call | solution.py:131
Async XLA Ops:
  0.0 0.9 %copy-start = (bf16[4,128,128]{2,1,0:T(8,128)(2,1)S(1)}, bf16[4,128,128]{2,1,0:T(8,128)(2,1)}, u32[]{:S(2)}) copy-start(bf16[4,128,128]{2,1,0:T(8,128)(2,1)} %param.5) | copy-start | bytes 393220
  0.0 1.8 %copy-start.2 = (f32[41,128]{1,0:T(8,128)S(1)}, f32[41,128]{1,0:T(8,128)}, u32[]{:S(2)}) copy-start(f32[41,128]{1,0:T(8,128)} %kx_ref.1) | copy-start | bytes 62980
  1.9 2.4 %copy-start.1 = (bf16[1,128,256]{2,1,0:T(8,128)(2,1)S(1)}, bf16[1,128,256]{2,1,0:T(8,128)(2,1)}, u32[]{:S(2)}) copy-start(bf16[1,128,256]{2,1,0:T(8,128)(2,1)} %b_ref.1) | copy-start | bytes 196612
  2.8 1.5 %collective-permute-start = (bf16[4,128,128]{2,1,0:T(8,128)(2,1)S(1)}, bf16[4,128,128]{2,1,0:T(8,128)(2,1)S(1)}, u32[]{:S(2)}, u32[]{:S(2)}) collective-permute-start(bf16[4,128,128]{2,1,0:T(8,128)(2,1)S(1)} %shard_map.55.z_ref), channel_id=1, source_target_pairs={{0,1},{1,0},{2,3},{3,2},{4,5},{5,4},{6,7},{7,6},{8,9},{9,8},{10,11... | collective-permute-start | bytes 393224 | tf_op jit(solution)/shard_map/ppermute | solution.py:150
  3.3 1.0 %copy-start.4 = (s32[4,128]{1,0:T(4,128)S(1)}, s32[4,128]{1,0:T(4,128)}, u32[]{:S(2)}) copy-start(s32[4,128]{1,0:T(4,128)} %sea_ref.1) | copy-start | bytes 6148
  4.6 14.3 %copy-start.3 = (f32[41,128]{1,0:T(8,128)S(1)}, f32[41,128]{1,0:T(8,128)}, u32[]{:S(2)}) copy-start(f32[41,128]{1,0:T(8,128)} %ky_ref.1) | copy-start | bytes 62980

commit v12 on v11

--- a/solution.py
+++ b/solution.py
@@ -144,7 +144,7 @@
 def per_device(nt, increment, land_sea, kernel_x, kernel_y, balance):
     rows, nx, _ = increment.shape
     on_diagonal = lax.broadcasted_iota(jnp.int32, (rows, nx, nx), 1) == lax.broadcasted_iota(jnp.int32, (rows, nx, nx), 2)
-    diag = jnp.where(on_diagonal, land_sea[:, :, None], 0).astype(increment.dtype)
+    diag = lax.optimization_barrier(jnp.where(on_diagonal, land_sea[:, :, None], 0).astype(increment.dtype))
     masked = jnp.einsum("rxy,ryc->rxc", diag, increment, preferred_element_type=F32).astype(increment.dtype)
     z = zonal(masked, kernel_x)
     z_other = lax.ppermute(z, "comp", [(0, 1), (1, 0)])

time: 20.4 us -> 20.2 us (level)
  other arithmetic: 0 us -> 0.85 us
  matrix products: 0.93 us -> 0.17 us
  local copies, waits for them, and re-layouts: 0.92 us -> 0.64 us
    convert_element_type x0 -> x1, other arithmetic: none -> 0.85 us  [per_device(): jnp.where(on_diagonal, land_sea[:, :, None], 0).astype(increment.dtype)]
    dot_general x1, matrix products: 0.93 us -> 0.17 us  [per_device(): jnp.einsum('rxy,ryc->rxc', diag, increment, preferred_element_type=F32)]
    unnamed x10, local copies, waits for them, and re-layouts: 0.92 us -> 0.64 us
where the time goes in v12:
time: 20.2 us; the launch traced here: 20 us
  blocking collectives  14.3 us (71%)
  Pallas kernels  2.43 us (12%)
  waiting for transfers between devices  0.98 us (5%)
  other arithmetic  0.85 us (4%)
  local copies, waits for them, and re-layouts  0.64 us (3%)
  starting transfers between devices  0.52 us (3%)
    all_to_all x1, blocking collectives, per_device(): lax.all_to_all(mixed, 'tile', split_axis=0, concat_axis=0, tiled=True)  14.3 us
    pallas_call x1, Pallas kernels, meridional(): pl.pallas_call(meridional_kernel, out_shape=jax.ShapeDtypeStruct(m.shape,...  1.22 us
    ppermute x1, waiting for transfers between devices, per_device(): z_other = lax.ppermute(z, 'comp', [(0, 1), (1, 0)])  0.98 us
    pallas_call x1, Pallas kernels, zonal(): pl.pallas_call(zonal_kernel, out_shape=jax.ShapeDtypeStruct(m.shape, BF16...  0.88 us
    convert_element_type x1, other arithmetic, per_device(): jnp.where(on_diagonal, land_sea[:, :, None], 0).astype(increment.dtype)  0.85 us
    unnamed x10, local copies, waits for them, and re-layouts  0.64 us
    ppermute x1, starting transfers between devices, per_device(): z_other = lax.ppermute(z, 'comp', [(0, 1), (1, 0)])  0.52 us
  transfers between devices with their start and end apart: 1, of which 1 were waited for; matrix products, arithmetic and copies ran while one was open for 0% of the time, Pallas kernels for 0%

profile of v12, /device:TPU:0, one launch (start us, length us, event | category | flops | bytes accessed | tf_op | source)
XLA Modules:
  0.0 20.0 jit_solution(6355068240435549644)
XLA Ops:
  0.0 0.0 copy-start
  0.0 0.8 %select_convert_fusion = bf16[4,128,128]{2,1,0:T(8,128)(2,1)S(1)} fusion(s32[4,128]{1,0:T(4,128)} %sea_ref.1), kind=kLoop, calls=%fused_computation.1 | loop fusion | flops 196608 | bytes 133120 | tf_op jit(solution)/shard_map/convert_element_type | solution.py:147
  0.9 0.1 copy-done
  0.9 0.0 copy-start.2
  0.9 0.2 convolution_convert_fusion.m_ref
  1.1 0.6 %copy-done.2 = f32[41,128]{1,0:T(8,128)S(1)} copy-done((f32[41,128]{1,0:T(8,128)S(1)}, f32[41,128]{1,0:T(8,128)}, u32[]{:S(2)}) %copy-start.2) | copy-done | bytes 21016
  1.7 0.0 copy-start.1
  1.7 0.9 %shard_map.55.z_ref = bf16[4,128,128]{2,1,0:T(8,128)(2,1)S(1)} custom-call(bf16[4,128,128]{2,1,0:T(8,128)(2,1)S(1)} %convolution_convert_fusion.m_ref, f32[41,128]{1,0:T(8,128)S(1)} %copy-done.2), custom_call_target="tpu_custom_call" | custom-call | flops 5373952 | bytes 262144 | tf_op jit(solution)/shard_map/pallas_call | solution.py:47
  2.5 0.5 %collective-permute-start = (bf16[4,128,128]{2,1,0:T(8,128)(2,1)S(1)}, bf16[4,128,128]{2,1,0:T(8,128)(2,1)S(1)}, u32[]{:S(2)}, u32[]{:S(2)}) collective-permute-start(bf16[4,128,128]{2,1,0:T(8,128)(2,1)S(1)} %shard_map.55.z_ref), channel_id=1, source_target_pairs={{0,1},{1,0},{2,3},{3,2},{4,5},{5,4},{6,7},{7,6},{8,9},{9,8},{10,11... | collective-permute-start | bytes 393224 | tf_op jit(solution)/shard_map/ppermute | solution.py:150
  3.1 0.0 copy-start.4
  3.1 1.0 %collective-permute-done.zo_ref = bf16[4,128,128]{2,1,0:T(8,128)(2,1)S(1)} collective-permute-done((bf16[4,128,128]{2,1,0:T(8,128)(2,1)S(1)}, bf16[4,128,128]{2,1,0:T(8,128)(2,1)S(1)}, u32[]{:S(2)}, u32[]{:S(2)}) %collective-permute-start) | collective-permute-done | bytes 131104 | tf_op jit(solution)/shard_map/ppermute | solution.py:150
  4.0 0.0 copy-done.1
  4.1 0.0 copy-done.4
  4.1 0.3 %shard_map.56 = bf16[8,4,16,128]{3,2,1,0:T(8,128)(2,1)S(1)} custom-call(s32[1]{0:T(128)} %bitcast.c_ref, bf16[4,128,128]{2,1,0:T(8,128)(2,1)S(1)} %shard_map.55.z_ref, bf16[4,128,128]{2,1,0:T(8,128)(2,1)S(1)} %collective-permute-done.zo_ref, bf16[1,128,256]{2,1,0:T(8,128)(2,1)S(1)} %copy-done.1, s32[4,128]{1,0:T(4,128)S(1)} %copy-done.4), custom_call_target="tpu_custom_call" | custom-call | flops 33554432 | bytes 458752 | tf_op jit(solution)/shard_map/pallas_call | solution.py:81
  4.4 0.0 copy-start.3
  4.4 14.3 %all_to_all.5 = bf16[8,4,16,128]{3,2,1,0:T(8,128)(2,1)S(1)} all-to-all(bf16[8,4,16,128]{3,2,1,0:T(8,128)(2,1)S(1)} %shard_map.56), channel_id=1, replica_groups=mesh['ens'=2,'tile'=8,'comp'=2] {'tile'}, dimensions={0} | all-to-all | bytes 262144 | tf_op jit(solution)/shard_map/all_to_all | solution.py:153
  18.7 0.0 copy-done.3
  18.7 1.2 %shard_map.57 = bf16[32,16,128]{2,1,0:T(8,128)(2,1)} custom-call(bf16[32,16,128]{2,1,0:T(8,128)(2,1)S(1)} %bitcast.4, f32[41,128]{1,0:T(8,128)S(1)} %copy-done.3), custom_call_target="tpu_custom_call" | custom-call | flops 5373952 | bytes 262144 | tf_op jit(solution)/shard_map/pallas_call | solution.py:131
Async XLA Ops:
  0.0 0.9 %copy-start = (bf16[4,128,128]{2,1,0:T(8,128)(2,1)S(1)}, bf16[4,128,128]{2,1,0:T(8,128)(2,1)}, u32[]{:S(2)}) copy-start(bf16[4,128,128]{2,1,0:T(8,128)(2,1)} %param.5) | copy-start | bytes 393220
  0.9 0.7 %copy-start.2 = (f32[41,128]{1,0:T(8,128)S(1)}, f32[41,128]{1,0:T(8,128)}, u32[]{:S(2)}) copy-start(f32[41,128]{1,0:T(8,128)} %kx_ref.1) | copy-start | bytes 62980
  1.7 2.4 %copy-start.1 = (bf16[1,128,256]{2,1,0:T(8,128)(2,1)S(1)}, bf16[1,128,256]{2,1,0:T(8,128)(2,1)}, u32[]{:S(2)}) copy-start(bf16[1,128,256]{2,1,0:T(8,128)(2,1)} %b_ref.1) | copy-start | bytes 196612
  2.5 1.5 %collective-permute-start = (bf16[4,128,128]{2,1,0:T(8,128)(2,1)S(1)}, bf16[4,128,128]{2,1,0:T(8,128)(2,1)S(1)}, u32[]{:S(2)}, u32[]{:S(2)}) collective-permute-start(bf16[4,128,128]{2,1,0:T(8,128)(2,1)S(1)} %shard_map.55.z_ref), channel_id=1, source_target_pairs={{0,1},{1,0},{2,3},{3,2},{4,5},{5,4},{6,7},{7,6},{8,9},{9,8},{10,11... | collective-permute-start | bytes 393224 | tf_op jit(solution)/shard_map/ppermute | solution.py:150
  3.1 1.0 %copy-start.4 = (s32[4,128]{1,0:T(4,128)S(1)}, s32[4,128]{1,0:T(4,128)}, u32[]{:S(2)}) copy-start(s32[4,128]{1,0:T(4,128)} %sea_ref.1) | copy-start | bytes 6148
  4.4 14.4 %copy-start.3 = (f32[41,128]{1,0:T(8,128)S(1)}, f32[41,128]{1,0:T(8,128)}, u32[]{:S(2)}) copy-start(f32[41,128]{1,0:T(8,128)} %ky_ref.1) | copy-start | bytes 62980

commit v13 on v9

--- a/solution.py
+++ b/solution.py
@@ -166,7 +166,10 @@
 
 
 def per_device(nt, increment, land_sea, kernel_x, kernel_y, balance):
-    masked = increment * land_sea.astype(increment.dtype)[:, :, None]
+    rows, nx, _ = increment.shape
+    on_diagonal = lax.broadcasted_iota(jnp.int32, (rows, nx, nx), 1) == lax.broadcasted_iota(jnp.int32, (rows, nx, nx), 2)
+    diag = lax.optimization_barrier(jnp.where(on_diagonal, land_sea[:, :, None], 0).astype(increment.dtype))
+    masked = jnp.einsum("rxy,ryc->rxc", diag, increment, preferred_element_type=F32).astype(increment.dtype)
     z = zonal(masked, kernel_x)
     z_other = lax.ppermute(z, "comp", [(0, 1), (1, 0)])
     c = lax.axis_index("comp").astype(jnp.int32).reshape(1)

time: 20.2 us -> 20.2 us (level)
  other arithmetic: 1.72 us -> 0.85 us
  local copies, waits for them, and re-layouts: 0.02 us -> 0.63 us
    mul x1 -> x0, other arithmetic: 1.04 us -> none  [per_device(): masked = increment * land_sea.astype(increment.dtype)[:, :, None]]
    unnamed x8 -> x10, local copies, waits for them, and re-layouts: 0.02 us -> 0.63 us
where the time goes in v13:
time: 20.2 us; the launch traced here: 19.9 us
  blocking collectives  14.3 us (71%)
  Pallas kernels  2.58 us (13%)
  other arithmetic  0.85 us (4%)
  waiting for transfers between devices  0.77 us (4%)
  local copies, waits for them, and re-layouts  0.63 us (3%)
  starting transfers between devices  0.52 us (3%)
    all_to_all x1, blocking collectives, per_device(): lax.all_to_all(mixed, 'tile', split_axis=0, concat_axis=0, tiled=True)  14.3 us
    pallas_call x1, Pallas kernels, meridional(): pl.pallas_call(meridional_kernel, out_shape=jax.ShapeDtypeStruct(m.shape,...  1.15 us
    pallas_call x1, Pallas kernels, zonal(): pl.pallas_call(zonal_kernel, out_shape=jax.ShapeDtypeStruct(m.shape, BF16...  0.93 us
    convert_element_type x1, other arithmetic, per_device(): jnp.where(on_diagonal, land_sea[:, :, None], 0).astype(increment.dtype)  0.85 us
    ppermute x1, waiting for transfers between devices, per_device(): z_other = lax.ppermute(z, 'comp', [(0, 1), (1, 0)])  0.77 us
    unnamed x10, local copies, waits for them, and re-layouts  0.63 us
    ppermute x1, starting transfers between devices, per_device(): z_other = lax.ppermute(z, 'comp', [(0, 1), (1, 0)])  0.52 us
  transfers between devices with their start and end apart: 1, of which 1 were waited for; matrix products, arithmetic and copies ran while one was open for 0% of the time, Pallas kernels for 1%

profile of v13, /device:TPU:0, one launch (start us, length us, event | category | flops | bytes accessed | tf_op | source)
XLA Modules:
  0.0 19.9 jit_solution(4153111990483419005)
XLA Ops:
  0.0 0.0 copy-start
  0.0 0.8 %select_convert_fusion = bf16[4,128,128]{2,1,0:T(8,128)(2,1)S(1)} fusion(s32[4,128]{1,0:T(4,128)} %sea_ref.1), kind=kLoop, calls=%fused_computation.1 | loop fusion | flops 196608 | bytes 133120 | tf_op jit(solution)/shard_map/convert_element_type | solution.py:171
  0.9 0.1 copy-done
  0.9 0.0 copy-start.2
  0.9 0.2 convolution_convert_fusion.m_ref
  1.1 0.6 %copy-done.2 = f32[41,128]{1,0:T(8,128)S(1)} copy-done((f32[41,128]{1,0:T(8,128)S(1)}, f32[41,128]{1,0:T(8,128)}, u32[]{:S(2)}) %copy-start.2) | copy-done | bytes 21016
  1.7 0.0 copy-start.1
  1.7 0.9 %shard_map.55.z_ref = bf16[4,128,128]{2,1,0:T(8,128)(2,1)S(1)} custom-call(bf16[4,128,128]{2,1,0:T(8,128)(2,1)S(1)} %convolution_convert_fusion.m_ref, f32[41,128]{1,0:T(8,128)S(1)} %copy-done.2), custom_call_target="tpu_custom_call" | custom-call | flops 5373952 | bytes 262144 | tf_op jit(solution)/shard_map/pallas_call | solution.py:47
  2.6 0.5 %collective-permute-start = (bf16[4,128,128]{2,1,0:T(8,128)(2,1)S(1)}, bf16[4,128,128]{2,1,0:T(8,128)(2,1)S(1)}, u32[]{:S(2)}, u32[]{:S(2)}) collective-permute-start(bf16[4,128,128]{2,1,0:T(8,128)(2,1)S(1)} %shard_map.55.z_ref), channel_id=1, source_target_pairs={{0,1},{1,0},{2,3},{3,2},{4,5},{5,4},{6,7},{7,6},{8,9},{9,8},{10,11... | collective-permute-start | bytes 393224 | tf_op jit(solution)/shard_map/ppermute | solution.py:174
  3.1 0.0 copy-done.1
  3.1 0.0 copy-start.4
  3.1 0.2 shard_map.56.p_ref
  3.3 0.8 %collective-permute-done.zo_ref = bf16[4,128,128]{2,1,0:T(8,128)(2,1)S(1)} collective-permute-done((bf16[4,128,128]{2,1,0:T(8,128)(2,1)S(1)}, bf16[4,128,128]{2,1,0:T(8,128)(2,1)S(1)}, u32[]{:S(2)}, u32[]{:S(2)}) %collective-permute-start) | collective-permute-done | bytes 131104 | tf_op jit(solution)/shard_map/ppermute | solution.py:174
  4.1 0.0 copy-done.4
  4.1 0.3 %shard_map.57 = bf16[8,4,16,128]{3,2,1,0:T(8,128)(2,1)S(1)} custom-call(s32[1]{0:T(128)} %bitcast.c_ref, f32[4,128,128]{2,1,0:T(8,128)S(1)} %shard_map.56.p_ref, bf16[4,128,128]{2,1,0:T(8,128)(2,1)S(1)} %collective-permute-done.zo_ref, bf16[1,128,256]{2,1,0:T(8,128)(2,1)S(1)} %copy-done.1, s32[4,128]{1,0:T(4,128)S(1)} %copy-done.4), custom_call_target="tpu_custom_call" | custom-call | flops 16777216 | bytes 589824 | tf_op jit(solution)/shard_map/pallas_call | solution.py:100
  4.4 0.0 copy-start.3
  4.4 14.3 %all_to_all.5 = bf16[8,4,16,128]{3,2,1,0:T(8,128)(2,1)S(1)} all-to-all(bf16[8,4,16,128]{3,2,1,0:T(8,128)(2,1)S(1)} %shard_map.57), channel_id=1, replica_groups=mesh['ens'=2,'tile'=8,'comp'=2] {'tile'}, dimensions={0} | all-to-all | bytes 262144 | tf_op jit(solution)/shard_map/all_to_all | solution.py:177
  18.7 0.0 copy-done.3
  18.8 1.2 %shard_map.58 = bf16[32,16,128]{2,1,0:T(8,128)(2,1)} custom-call(bf16[32,16,128]{2,1,0:T(8,128)(2,1)S(1)} %bitcast.4, f32[41,128]{1,0:T(8,128)S(1)} %copy-done.3), custom_call_target="tpu_custom_call" | custom-call | flops 5373952 | bytes 262144 | tf_op jit(solution)/shard_map/pallas_call | solution.py:155
Async XLA Ops:
  0.0 0.9 %copy-start = (bf16[4,128,128]{2,1,0:T(8,128)(2,1)S(1)}, bf16[4,128,128]{2,1,0:T(8,128)(2,1)}, u32[]{:S(2)}) copy-start(bf16[4,128,128]{2,1,0:T(8,128)(2,1)} %param.5) | copy-start | bytes 393220
  0.9 0.7 %copy-start.2 = (f32[41,128]{1,0:T(8,128)S(1)}, f32[41,128]{1,0:T(8,128)}, u32[]{:S(2)}) copy-start(f32[41,128]{1,0:T(8,128)} %kx_ref.1) | copy-start | bytes 62980
  1.7 1.5 %copy-start.1 = (bf16[1,128,256]{2,1,0:T(8,128)(2,1)S(1)}, bf16[1,128,256]{2,1,0:T(8,128)(2,1)}, u32[]{:S(2)}) copy-start(bf16[1,128,256]{2,1,0:T(8,128)(2,1)} %b_ref.3) | copy-start | bytes 196612
  2.6 1.5 %collective-permute-start = (bf16[4,128,128]{2,1,0:T(8,128)(2,1)S(1)}, bf16[4,128,128]{2,1,0:T(8,128)(2,1)S(1)}, u32[]{:S(2)}, u32[]{:S(2)}) collective-permute-start(bf16[4,128,128]{2,1,0:T(8,128)(2,1)S(1)} %shard_map.55.z_ref), channel_id=1, source_target_pairs={{0,1},{1,0},{2,3},{3,2},{4,5},{5,4},{6,7},{7,6},{8,9},{9,8},{10,11... | collective-permute-start | bytes 393224 | tf_op jit(solution)/shard_map/ppermute | solution.py:174
  3.1 1.0 %copy-start.4 = (s32[4,128]{1,0:T(4,128)S(1)}, s32[4,128]{1,0:T(4,128)}, u32[]{:S(2)}) copy-start(s32[4,128]{1,0:T(4,128)} %sea_ref.1) | copy-start | bytes 6148
  4.4 14.3 %copy-start.3 = (f32[41,128]{1,0:T(8,128)S(1)}, f32[41,128]{1,0:T(8,128)}, u32[]{:S(2)}) copy-start(f32[41,128]{1,0:T(8,128)} %ky_ref.1) | copy-start | bytes 62980

commit v14 on v6

--- a/solution.py
+++ b/solution.py
@@ -100,7 +100,7 @@
     pad_ref[0:half] = jnp.zeros((half, w, ch), F32)
     pad_ref[half + ny :] = jnp.zeros((half, w, ch), F32)
     pad_ref[half : half + ny] = m_ref[...].astype(F32)
-    chunk = min(ny, 8)
+    chunk = min(ny, 2)
     n_chunks = ny // chunk
 
     def rows_at(y0, lo, hi):
@@ -109,7 +109,7 @@
             acc = acc + ky_ref[k : k + 1, :][None] * pad_ref[pl.ds(y0 + k, chunk)]
         out_ref[pl.ds(y0, chunk)] = acc.astype(out_ref.dtype)
 
-    if n_chunks <= 8:
+    if n_chunks <= 16:
         for c in range(n_chunks):
             y0 = c * chunk
             lo = max(0, half - y0 - chunk + 1)

time: 20.3 us -> 20.2 us (level)
  no operation moved by 1% of the time
where the time goes in v14:
time: 20.2 us; the launch traced here: 20 us
  blocking collectives  14.3 us (71%)
  Pallas kernels  2.37 us (12%)
  other arithmetic  1.72 us (9%)
  waiting for transfers between devices  0.98 us (5%)
  starting transfers between devices  0.52 us (3%)
    all_to_all x1, blocking collectives, per_device(): lax.all_to_all(mixed, 'tile', split_axis=0, concat_axis=0, tiled=True)  14.3 us
    pallas_call x1, Pallas kernels, meridional(): pl.pallas_call(meridional_kernel, out_shape=jax.ShapeDtypeStruct(m.shape,...  1.16 us
    mul x1, other arithmetic, per_device(): masked = increment * land_sea.astype(increment.dtype)[:, :, None]  1.04 us
    ppermute x1, waiting for transfers between devices, per_device(): z_other = lax.ppermute(z, 'comp', [(0, 1), (1, 0)])  0.98 us
    pallas_call x1, Pallas kernels, zonal(): pl.pallas_call(zonal_kernel, out_shape=jax.ShapeDtypeStruct(m.shape, BF16...  0.88 us
    convert_element_type x1, other arithmetic, per_device(): masked = increment * land_sea.astype(increment.dtype)[:, :, None]  0.68 us
    ppermute x1, starting transfers between devices, per_device(): z_other = lax.ppermute(z, 'comp', [(0, 1), (1, 0)])  0.52 us
  transfers between devices with their start and end apart: 1, of which 1 were waited for; matrix products, arithmetic and copies ran while one was open for 0% of the time, Pallas kernels for 0%

profile of v14, /device:TPU:0, one launch (start us, length us, event | category | flops | bytes accessed | tf_op | source)
XLA Modules:
  0.0 20.0 jit_solution(9778188559831874744)
XLA Ops:
  0.0 0.7 %convert_element_type.3 = bf16[4,128]{1,0:T(4,128)(2,1)S(1)} convert(s32[4,128]{1,0:T(4,128)} %sea_ref.1) | non-fusion elementwise | flops 512 | bytes 3072 | tf_op jit(solution)/shard_map/convert_element_type | solution.py:145
  0.7 0.0 copy-start.1
  0.7 1.0 %broadcast_multiply_fusion.m_ref = bf16[4,128,128]{2,1,0:T(8,128)(2,1)S(1)} fusion(bf16[4,128,128]{2,1,0:T(8,128)(2,1)} %param.5, bf16[4,128]{1,0:T(4,128)(2,1)S(1)} %convert_element_type.3), kind=kLoop, calls=%fused_computation | loop fusion | flops 65536 | bytes 263168 | tf_op jit(solution)/shard_map/mul | solution.py:145
  1.7 0.0 copy-done.1
  1.7 0.0 copy-start
  1.8 0.9 %shard_map.55.z_ref = bf16[4,128,128]{2,1,0:T(8,128)(2,1)S(1)} custom-call(bf16[4,128,128]{2,1,0:T(8,128)(2,1)S(1)} %broadcast_multiply_fusion.m_ref, f32[41,128]{1,0:T(8,128)S(1)} %copy-done.1), custom_call_target="tpu_custom_call" | custom-call | flops 5373952 | bytes 262144 | tf_op jit(solution)/shard_map/pallas_call | solution.py:47
  2.6 0.5 %collective-permute-start = (bf16[4,128,128]{2,1,0:T(8,128)(2,1)S(1)}, bf16[4,128,128]{2,1,0:T(8,128)(2,1)S(1)}, u32[]{:S(2)}, u32[]{:S(2)}) collective-permute-start(bf16[4,128,128]{2,1,0:T(8,128)(2,1)S(1)} %shard_map.55.z_ref), channel_id=1, source_target_pairs={{0,1},{1,0},{2,3},{3,2},{4,5},{5,4},{6,7},{7,6},{8,9},{9,8},{10,11... | collective-permute-start | bytes 393224 | tf_op jit(solution)/shard_map/ppermute | solution.py:147
  3.2 0.0 copy-start.3
  3.2 1.0 %collective-permute-done.zo_ref = bf16[4,128,128]{2,1,0:T(8,128)(2,1)S(1)} collective-permute-done((bf16[4,128,128]{2,1,0:T(8,128)(2,1)S(1)}, bf16[4,128,128]{2,1,0:T(8,128)(2,1)S(1)}, u32[]{:S(2)}, u32[]{:S(2)}) %collective-permute-start) | collective-permute-done | bytes 131104 | tf_op jit(solution)/shard_map/ppermute | solution.py:147
  4.1 0.0 copy-done
  4.2 0.0 copy-done.3
  4.2 0.3 %shard_map.56 = bf16[8,4,16,128]{3,2,1,0:T(8,128)(2,1)S(1)} custom-call(s32[1]{0:T(128)} %bitcast.c_ref, bf16[4,128,128]{2,1,0:T(8,128)(2,1)S(1)} %shard_map.55.z_ref, bf16[4,128,128]{2,1,0:T(8,128)(2,1)S(1)} %collective-permute-done.zo_ref, bf16[1,128,256]{2,1,0:T(8,128)(2,1)S(1)} %copy-done, s32[4,128]{1,0:T(4,128)S(1)} %copy-done.3), custom_call_target="tpu_custom_call" | custom-call | flops 33554432 | bytes 458752 | tf_op jit(solution)/shard_map/pallas_call | solution.py:81
  4.5 0.0 copy-start.2
  4.5 14.3 %all_to_all.5 = bf16[8,4,16,128]{3,2,1,0:T(8,128)(2,1)S(1)} all-to-all(bf16[8,4,16,128]{3,2,1,0:T(8,128)(2,1)S(1)} %shard_map.56), channel_id=1, replica_groups=mesh['ens'=2,'tile'=8,'comp'=2] {'tile'}, dimensions={0} | all-to-all | bytes 262144 | tf_op jit(solution)/shard_map/all_to_all | solution.py:150
  18.8 0.0 copy-done.2
  18.8 1.2 %shard_map.57 = bf16[32,16,128]{2,1,0:T(8,128)(2,1)} custom-call(bf16[32,16,128]{2,1,0:T(8,128)(2,1)S(1)} %bitcast.2, f32[41,128]{1,0:T(8,128)S(1)} %copy-done.2), custom_call_target="tpu_custom_call" | custom-call | flops 5373952 | bytes 262144 | tf_op jit(solution)/shard_map/pallas_call | solution.py:131
Async XLA Ops:
  0.7 1.1 %copy-start.1 = (f32[41,128]{1,0:T(8,128)S(1)}, f32[41,128]{1,0:T(8,128)}, u32[]{:S(2)}) copy-start(f32[41,128]{1,0:T(8,128)} %kx_ref.1) | copy-start | bytes 62980
  1.7 2.4 %copy-start = (bf16[1,128,256]{2,1,0:T(8,128)(2,1)S(1)}, bf16[1,128,256]{2,1,0:T(8,128)(2,1)}, u32[]{:S(2)}) copy-start(bf16[1,128,256]{2,1,0:T(8,128)(2,1)} %b_ref.1) | copy-start | bytes 196612
  2.6 1.5 %collective-permute-start = (bf16[4,128,128]{2,1,0:T(8,128)(2,1)S(1)}, bf16[4,128,128]{2,1,0:T(8,128)(2,1)S(1)}, u32[]{:S(2)}, u32[]{:S(2)}) collective-permute-start(bf16[4,128,128]{2,1,0:T(8,128)(2,1)S(1)} %shard_map.55.z_ref), channel_id=1, source_target_pairs={{0,1},{1,0},{2,3},{3,2},{4,5},{5,4},{6,7},{7,6},{8,9},{9,8},{10,11... | collective-permute-start | bytes 393224 | tf_op jit(solution)/shard_map/ppermute | solution.py:147
  3.2 1.0 %copy-start.3 = (s32[4,128]{1,0:T(4,128)S(1)}, s32[4,128]{1,0:T(4,128)}, u32[]{:S(2)}) copy-start(s32[4,128]{1,0:T(4,128)} %sea_ref.1) | copy-start | bytes 6148
  4.5 14.3 %copy-start.2 = (f32[41,128]{1,0:T(8,128)S(1)}, f32[41,128]{1,0:T(8,128)}, u32[]{:S(2)}) copy-start(f32[41,128]{1,0:T(8,128)} %ky_ref.1) | copy-start | bytes 62980

commit v15 on v13

--- a/solution.py
+++ b/solution.py
@@ -116,36 +116,31 @@
     ny, w, ch = m_ref.shape
     taps = ky_ref.shape[0]
     half = (taps - 1) // 2
-    chunk = min(ny, 8)
-    n_chunks = ny // chunk
-    if n_chunks <= 8:
-        pad_ref[0:ny] = m_ref[...].astype(F32)
-        for c in range(n_chunks):
-            y0 = c * chunk
-            acc = [None] * chunk
-            for k in range(taps):
-                d = k - half
-                lo, hi = max(0, -d - y0), min(chunk, ny - d - y0)
-                if lo >= hi:
-                    continue
-                term = ky_ref[k : k + 1, :][None] * pad_ref[y0 + d + lo : y0 + d + hi]
-                for y in range(lo, hi):
-                    acc[y] = term[y - lo] if acc[y] is None else acc[y] + term[y - lo]
-            out_ref[y0 : y0 + chunk] = jnp.stack(acc).astype(out_ref.dtype)
-        return
     pad_ref[0:half] = jnp.zeros((half, w, ch), F32)
     pad_ref[half + ny :] = jnp.zeros((half, w, ch), F32)
     pad_ref[half : half + ny] = m_ref[...].astype(F32)
+    chunk = min(ny, 2)
+    n_chunks = ny // chunk
 
-    def body(i, carry):
-        y0 = pl.multiple_of(i * chunk, chunk)
+    def rows_at(y0, lo, hi):
         acc = jnp.zeros((chunk, w, ch), F32)
-        for k in range(taps):
+        for k in range(lo, hi):
             acc = acc + ky_ref[k : k + 1, :][None] * pad_ref[pl.ds(y0 + k, chunk)]
         out_ref[pl.ds(y0, chunk)] = acc.astype(out_ref.dtype)
-        return carry
 
-    lax.fori_loop(0, n_chunks, body, 0)
+    if n_chunks <= 16:
+        for c in range(n_chunks):
+            y0 = c * chunk
+            lo = max(0, half - y0 - chunk + 1)
+            hi = min(taps, half + ny - y0)
+            rows_at(y0, lo, hi)
+    else:
+
+        def body(i, carry):
+            rows_at(pl.multiple_of(i * chunk, chunk), 0, taps)
+            return carry
+
+        lax.fori_loop(0, n_chunks, body, 0)
 
 
 def meridional(m, ky):

time: 20.2 us -> 20.2 us (level)
  no operation moved by 1% of the time
where the time goes in v15:
time: 20.2 us; the launch traced here: 19.9 us
  blocking collectives  14.3 us (71%)
  Pallas kernels  2.58 us (13%)
  other arithmetic  0.85 us (4%)
  waiting for transfers between devices  0.77 us (4%)
  local copies, waits for them, and re-layouts  0.63 us (3%)
  starting transfers between devices  0.52 us (3%)
    all_to_all x1, blocking collectives, per_device(): lax.all_to_all(mixed, 'tile', split_axis=0, concat_axis=0, tiled=True)  14.3 us
    pallas_call x1, Pallas kernels, meridional(): pl.pallas_call(meridional_kernel, out_shape=jax.ShapeDtypeStruct(m.shape,...  1.16 us
    pallas_call x1, Pallas kernels, zonal(): pl.pallas_call(zonal_kernel, out_shape=jax.ShapeDtypeStruct(m.shape, BF16...  0.93 us
    convert_element_type x1, other arithmetic, per_device(): jnp.where(on_diagonal, land_sea[:, :, None], 0).astype(increment.dtype)  0.85 us
    ppermute x1, waiting for transfers between devices, per_device(): z_other = lax.ppermute(z, 'comp', [(0, 1), (1, 0)])  0.77 us
    unnamed x10, local copies, waits for them, and re-layouts  0.63 us
    ppermute x1, starting transfers between devices, per_device(): z_other = lax.ppermute(z, 'comp', [(0, 1), (1, 0)])  0.52 us
  transfers between devices with their start and end apart: 1, of which 1 were waited for; matrix products, arithmetic and copies ran while one was open for 0% of the time, Pallas kernels for 1%

profile of v15, /device:TPU:0, one launch (start us, length us, event | category | flops | bytes accessed | tf_op | source)
XLA Modules:
  0.0 19.9 jit_solution(16502750751242560516)
XLA Ops:
  0.0 0.0 copy-start
  0.0 0.8 %select_convert_fusion = bf16[4,128,128]{2,1,0:T(8,128)(2,1)S(1)} fusion(s32[4,128]{1,0:T(4,128)} %sea_ref.1), kind=kLoop, calls=%fused_computation.1 | loop fusion | flops 196608 | bytes 133120 | tf_op jit(solution)/shard_map/convert_element_type | solution.py:166
  0.9 0.1 copy-done
  0.9 0.0 copy-start.2
  0.9 0.2 convolution_convert_fusion.m_ref
  1.1 0.6 %copy-done.2 = f32[41,128]{1,0:T(8,128)S(1)} copy-done((f32[41,128]{1,0:T(8,128)S(1)}, f32[41,128]{1,0:T(8,128)}, u32[]{:S(2)}) %copy-start.2) | copy-done | bytes 21016
  1.7 0.0 copy-start.1
  1.7 0.9 %shard_map.55.z_ref = bf16[4,128,128]{2,1,0:T(8,128)(2,1)S(1)} custom-call(bf16[4,128,128]{2,1,0:T(8,128)(2,1)S(1)} %convolution_convert_fusion.m_ref, f32[41,128]{1,0:T(8,128)S(1)} %copy-done.2), custom_call_target="tpu_custom_call" | custom-call | flops 5373952 | bytes 262144 | tf_op jit(solution)/shard_map/pallas_call | solution.py:47
  2.6 0.5 %collective-permute-start = (bf16[4,128,128]{2,1,0:T(8,128)(2,1)S(1)}, bf16[4,128,128]{2,1,0:T(8,128)(2,1)S(1)}, u32[]{:S(2)}, u32[]{:S(2)}) collective-permute-start(bf16[4,128,128]{2,1,0:T(8,128)(2,1)S(1)} %shard_map.55.z_ref), channel_id=1, source_target_pairs={{0,1},{1,0},{2,3},{3,2},{4,5},{5,4},{6,7},{7,6},{8,9},{9,8},{10,11... | collective-permute-start | bytes 393224 | tf_op jit(solution)/shard_map/ppermute | solution.py:169
  3.1 0.0 copy-done.1
  3.1 0.0 copy-start.4
  3.1 0.2 shard_map.56.p_ref
  3.3 0.8 %collective-permute-done.zo_ref = bf16[4,128,128]{2,1,0:T(8,128)(2,1)S(1)} collective-permute-done((bf16[4,128,128]{2,1,0:T(8,128)(2,1)S(1)}, bf16[4,128,128]{2,1,0:T(8,128)(2,1)S(1)}, u32[]{:S(2)}, u32[]{:S(2)}) %collective-permute-start) | collective-permute-done | bytes 131104 | tf_op jit(solution)/shard_map/ppermute | solution.py:169
  4.1 0.0 copy-done.4
  4.1 0.3 %shard_map.57 = bf16[8,4,16,128]{3,2,1,0:T(8,128)(2,1)S(1)} custom-call(s32[1]{0:T(128)} %bitcast.c_ref, f32[4,128,128]{2,1,0:T(8,128)S(1)} %shard_map.56.p_ref, bf16[4,128,128]{2,1,0:T(8,128)(2,1)S(1)} %collective-permute-done.zo_ref, bf16[1,128,256]{2,1,0:T(8,128)(2,1)S(1)} %copy-done.1, s32[4,128]{1,0:T(4,128)S(1)} %copy-done.4), custom_call_target="tpu_custom_call" | custom-call | flops 16777216 | bytes 589824 | tf_op jit(solution)/shard_map/pallas_call | solution.py:100
  4.4 0.0 copy-start.3
  4.4 14.3 %all_to_all.5 = bf16[8,4,16,128]{3,2,1,0:T(8,128)(2,1)S(1)} all-to-all(bf16[8,4,16,128]{3,2,1,0:T(8,128)(2,1)S(1)} %shard_map.57), channel_id=1, replica_groups=mesh['ens'=2,'tile'=8,'comp'=2] {'tile'}, dimensions={0} | all-to-all | bytes 262144 | tf_op jit(solution)/shard_map/all_to_all | solution.py:172
  18.7 0.0 copy-done.3
  18.8 1.2 %shard_map.58 = bf16[32,16,128]{2,1,0:T(8,128)(2,1)} custom-call(bf16[32,16,128]{2,1,0:T(8,128)(2,1)S(1)} %bitcast.4, f32[41,128]{1,0:T(8,128)S(1)} %copy-done.3), custom_call_target="tpu_custom_call" | custom-call | flops 5373952 | bytes 262144 | tf_op jit(solution)/shard_map/pallas_call | solution.py:150
Async XLA Ops:
  0.0 0.9 %copy-start = (bf16[4,128,128]{2,1,0:T(8,128)(2,1)S(1)}, bf16[4,128,128]{2,1,0:T(8,128)(2,1)}, u32[]{:S(2)}) copy-start(bf16[4,128,128]{2,1,0:T(8,128)(2,1)} %param.5) | copy-start | bytes 393220
  0.9 0.7 %copy-start.2 = (f32[41,128]{1,0:T(8,128)S(1)}, f32[41,128]{1,0:T(8,128)}, u32[]{:S(2)}) copy-start(f32[41,128]{1,0:T(8,128)} %kx_ref.1) | copy-start | bytes 62980
  1.7 1.5 %copy-start.1 = (bf16[1,128,256]{2,1,0:T(8,128)(2,1)S(1)}, bf16[1,128,256]{2,1,0:T(8,128)(2,1)}, u32[]{:S(2)}) copy-start(bf16[1,128,256]{2,1,0:T(8,128)(2,1)} %b_ref.3) | copy-start | bytes 196612
  2.6 1.5 %collective-permute-start = (bf16[4,128,128]{2,1,0:T(8,128)(2,1)S(1)}, bf16[4,128,128]{2,1,0:T(8,128)(2,1)S(1)}, u32[]{:S(2)}, u32[]{:S(2)}) collective-permute-start(bf16[4,128,128]{2,1,0:T(8,128)(2,1)S(1)} %shard_map.55.z_ref), channel_id=1, source_target_pairs={{0,1},{1,0},{2,3},{3,2},{4,5},{5,4},{6,7},{7,6},{8,9},{9,8},{10,11... | collective-permute-start | bytes 393224 | tf_op jit(solution)/shard_map/ppermute | solution.py:169
  3.1 1.0 %copy-start.4 = (s32[4,128]{1,0:T(4,128)S(1)}, s32[4,128]{1,0:T(4,128)}, u32[]{:S(2)}) copy-start(s32[4,128]{1,0:T(4,128)} %sea_ref.1) | copy-start | bytes 6148
  4.4 14.3 %copy-start.3 = (f32[41,128]{1,0:T(8,128)S(1)}, f32[41,128]{1,0:T(8,128)}, u32[]{:S(2)}) copy-start(f32[41,128]{1,0:T(8,128)} %ky_ref.1) | copy-start | bytes 62980
